TPU v7x, 128 devices: a whole 4x4x4 slice. The times are simulated.
128 devices in a mesh: wide: 16 (over x, z), narrow: 8 (over y, core).
Axes of the slice: x: 4, y: 4, z: 4, core: 2. Of those that a mesh axis runs over, the one named last changes fastest.
Arguments:
- tokens: bfloat16 [16384, 2048], P(('wide', 'narrow')), may hold values from -6 to 6
- queries: bfloat16 [16384, 2048], P(('wide', 'narrow')), may hold values from -5 to 5
- new_kv: bfloat16 [16384, 1024], P(('wide', 'narrow')), may hold values from -5 to 5
- page_pool: bfloat16 [2048, 64, 1024], P('wide', 'narrow'), may hold values from -5 to 5
- seg_ids: int32 [16, 1024], P('wide'), may hold values from 0 to 15, never falling along the last dimension, each value on 1 to 512 neighbouring positions
- cache_len: int32 [16, 16], P('wide'), may hold values from 64 to 512
- page_table: int32 [16, 16, 8], P('wide'), may hold values from 0 to 7, each once within a row
- moves: int32 [16], replicated, may hold values from 0 to 15, as said below
- out_weight: bfloat16 [2048, 2048], replicated, may hold values from -0.125 to 0.125
- norm_gain: float32 [2048], replicated, may hold values from 0.1 to 1.9
- expert_ids: int32 [16384, 6], P(('wide', 'narrow')), may hold values from 0 to 63, all different within a row; in each aligned block of 128 rows (0 to 127, 128 to 255, ...) at most 16 rows name the same one
- gate_weights: float32 [16384, 6], P(('wide', 'narrow')), may hold values from 0.05 to 0.35
- expert_in: bfloat16 [128, 2048, 1408], P(('wide', 'narrow')), may hold values from -0.125 to 0.125
- expert_out: bfloat16 [128, 704, 2048], P(('wide', 'narrow')), may hold values from -0.15625 to 0.15625
Outputs:
- layer_out: bfloat16 [16384, 2048], P(('wide', 'narrow'))
Inputs may be any that keep to these rules, and one draw needn't show every extreme that they name: Slot r of group g holds the request that slot r of group (g - moves[r]) mod 16 held before. No value appears more than 2 times, and some value appears exactly 2 times. The values 1, 15 and 8 each appear. `expert_ids`: within the 128 rows of one device no expert is named more than 16 times; in every draw some device names some expert exactly 16 times. `seg_ids`: never falling along a group's tokens; each of the 16 slots has one token or more. `page_table`: each row is a permutation.
All inputs are finite; a program needn't handle non-finite values.
Results may differ from a plain program's by a relative error of at most 0.006.
Values may be sent and summed in bfloat16 or wider, within the bound.
No kernel may reach another device: no remote copies, remote signals or barrier semaphores. Data moves between devices by JAX's collectives and lax.ppermute only.
A program may use at most 192 MiB of HBM per device.

v0:
```python
import functools

import jax
import jax.numpy as jnp
from jax import lax
from jax.experimental import pallas as pl
from jax.experimental.pallas import tpu as pltpu
from jax.sharding import Mesh
from jax.sharding import PartitionSpec as P

QH = 16
KVH = 4
HD = 128
TOPK = 6
PAGE_CAP = 2
NARROW = ("y", "core")
CHIPS = ("wide", "y")
WN = ("wide", "y", "core")


norm_eps = 1e-06
block_limit = 512
BQ = 128
BK = 128
LANES = 128


def rank_among_equal(values):
    length = values.shape[0]
    order = jnp.arange(length, dtype=jnp.int32)
    earlier = (values[None, :] == values[:, None]) & (order[None, :] < order[:, None])
    return jnp.sum(earlier.astype(jnp.int32), axis=1)


def block_scores(q_block, keys):
    return jnp.einsum("bhd,kd->hbk", q_block, keys, preferred_element_type=jnp.float32) * HD ** (
        -0.5
    )


def fresh_scores(start_row, q_heads, key_new, seg_all, block_len):
    q_block = lax.dynamic_slice_in_dim(q_heads, start_row, block_len, 0)
    seg_block = lax.dynamic_slice_in_dim(seg_all, start_row, block_len, 0)
    row_pos = start_row + jnp.arange(block_len, dtype=jnp.int32)
    positions = jnp.arange(seg_all.shape[0], dtype=jnp.int32)
    visible = (seg_block[:, None] == seg_all[None, :]) & (positions[None, :] <= row_pos[:, None])
    scores = jnp.where(visible[None], block_scores(q_block, key_new), -jnp.inf)
    return (q_block, seg_block, scores)


def attend_masked(
    start_row,
    q_heads,
    key_new,
    value_new,
    key_cached,
    value_cached,
    seg_all,
    lengths,
    cache_max,
    block_len,
):
    q_block, seg_block, fresh = fresh_scores(start_row, q_heads, key_new, seg_all, block_len)
    key_req = jnp.arange(key_cached.shape[0], dtype=jnp.int32) // cache_max
    key_pos = jnp.arange(key_cached.shape[0], dtype=jnp.int32) % cache_max
    visible = (seg_block[:, None] == key_req[None, :]) & (
        key_pos[None, :] < lengths[key_req][None, :]
    )
    older = jnp.where(visible[None], block_scores(q_block, key_cached), -jnp.inf)
    row_max = jnp.maximum(jnp.max(fresh, axis=-1), jnp.max(older, axis=-1))
    fresh_exp = jnp.exp(fresh - row_max[..., None])
    older_exp = jnp.exp(older - row_max[..., None])
    row_total = jnp.sum(fresh_exp, axis=-1) + jnp.sum(older_exp, axis=-1)
    fresh_w = (fresh_exp / row_total[..., None]).astype(jnp.bfloat16)
    older_w = (older_exp / row_total[..., None]).astype(jnp.bfloat16)
    attended = jnp.einsum("hbk,kd->bhd", fresh_w, value_new, preferred_element_type=jnp.float32)
    attended = attended + jnp.einsum(
        "hbk,kd->bhd", older_w, value_cached, preferred_element_type=jnp.float32
    )
    return attended.astype(jnp.bfloat16).reshape(block_len, -1)


def slot_attention(q_rows, kv_new, kv_cached, seg_all, lengths, cache_max):
    tokens = q_rows.shape[0]
    slots = lengths.shape[0]
    scale = HD ** (-0.5)
    n_q = tokens // BQ
    new_steps = (cache_max + BQ) // BK
    steps = new_steps + slots
    seg_start = jnp.sum(
        (seg_all[None, :] < jnp.arange(slots, dtype=jnp.int32)[:, None]).astype(jnp.int32), axis=1
    )
    firsts = seg_all[::BQ]
    lasts = seg_all[BQ - 1 :: BQ]
    kb_hi = (jnp.arange(n_q, dtype=jnp.int32) * BQ + BQ - 1) // BK
    kb_lo = jnp.maximum(seg_start[firsts] // BK, kb_hi - (new_steps - 1))
    n_new = kb_hi - kb_lo + 1
    n_old = lasts - firsts + 1
    t = jnp.arange(steps, dtype=jnp.int32)[None, :]
    new_idx = (kb_lo[:, None] + jnp.minimum(t, n_new[:, None] - 1)).reshape(-1)
    old_idx = (firsts[:, None] + jnp.clip(t - n_new[:, None], 0, n_old[:, None] - 1)).reshape(-1)
    counts = jnp.stack([n_new, n_old], axis=1).reshape(-1)
    q2 = q_rows.reshape(n_q, BQ, 2, HD).transpose(0, 2, 1, 3).reshape(n_q, 2 * BQ, HD)
    seg_q = jnp.broadcast_to(seg_all.reshape(n_q, 1, BQ, 1), (n_q, 2, BQ, LANES)).reshape(n_q, 2 * BQ, LANES)
    seg_k = jnp.broadcast_to(seg_all.reshape(tokens // BK, 1, BK), (tokens // BK, 8, BK))
    cached = kv_cached.reshape(slots, cache_max, 2 * HD)

    def kernel(new_sm, old_sm, cnt_sm, len_sm, q_ref, segq_ref, kn_ref, vn_ref, segk_ref, kc_ref, vc_ref, o_ref,
               m_ref, l_ref, acc_ref):
        b = pl.program_id(0)
        step = pl.program_id(1)
        nn = cnt_sm[2 * b]
        no = cnt_sm[2 * b + 1]

        @pl.when(step == 0)
        def _():
            m_ref[...] = jnp.full(m_ref.shape, -1e30, jnp.float32)
            l_ref[...] = jnp.zeros(l_ref.shape, jnp.float32)
            acc_ref[...] = jnp.zeros(acc_ref.shape, jnp.float32)

        def widen(x, width):
            return x if width == LANES else jnp.concatenate([x] * (width // LANES), axis=1)

        def visit(s, v):
            m = m_ref[...]
            m_new = jnp.maximum(m, jnp.max(s, axis=1, keepdims=True))
            alpha = jnp.exp(m - m_new)
            p = jnp.exp(s - widen(m_new, s.shape[1]))
            l_ref[...] = l_ref[...] * alpha + jnp.sum(p, axis=1, keepdims=True)
            acc_ref[...] = acc_ref[...] * alpha + jnp.dot(
                p.astype(jnp.bfloat16), v, preferred_element_type=jnp.float32)
            m_ref[...] = m_new

        q = q_ref[0]
        sq = segq_ref[0]

        @pl.when(step < nn)
        def _():
            kb = new_sm[b * steps + step]
            s = lax.dot_general(q, kn_ref[...], (((1,), (1,)), ((), ())),
                                preferred_element_type=jnp.float32) * scale
            rows = lax.broadcasted_iota(jnp.int32, s.shape, 0)
            cols = lax.broadcasted_iota(jnp.int32, s.shape, 1)
            qpos = b * BQ + jnp.bitwise_and(rows, BQ - 1)
            vis = (sq == segk_ref[0][:1, :]) & (kb * BK + cols <= qpos)
            visit(jnp.where(vis, s, -jnp.inf), vn_ref[...])

        @pl.when((step >= nn) & (step < nn + no))
        def _():
            r = old_sm[b * steps + step]
            s = lax.dot_general(q, kc_ref[0], (((1,), (1,)), ((), ())),
                                preferred_element_type=jnp.float32) * scale
            cols = lax.broadcasted_iota(jnp.int32, s.shape, 1)
            vis = (widen(sq, s.shape[1]) == r) & (cols < len_sm[r])
            visit(jnp.where(vis, s, -jnp.inf), vc_ref[0])

        @pl.when(step == steps - 1)
        def _():
            o_ref[0] = (acc_ref[...] / l_ref[...]).astype(jnp.bfloat16)

    def at(table):
        return lambda b, t, new_sm, old_sm, cnt_sm, len_sm: table(b, t, new_sm, old_sm)

    grid_spec = pltpu.PrefetchScalarGridSpec(
        num_scalar_prefetch=4,
        grid=(n_q, steps),
        in_specs=[
            pl.BlockSpec((1, 2 * BQ, HD), lambda b, t2, *_: (b, 0, 0)),
            pl.BlockSpec((1, 2 * BQ, LANES), lambda b, t2, *_: (b, 0, 0)),
            pl.BlockSpec((BK, HD), at(lambda b, t, n, o: (n[b * steps + t], 0))),
            pl.BlockSpec((BK, HD), at(lambda b, t, n, o: (n[b * steps + t], 1))),
            pl.BlockSpec((1, 8, BK), at(lambda b, t, n, o: (n[b * steps + t], 0, 0))),
            pl.BlockSpec((1, cache_max, HD), at(lambda b, t, n, o: (o[b * steps + t], 0, 0))),
            pl.BlockSpec((1, cache_max, HD), at(lambda b, t, n, o: (o[b * steps + t], 0, 1))),
        ],
        out_specs=pl.BlockSpec((1, 2 * BQ, HD), lambda b, t2, *_: (b, 0, 0)),
        scratch_shapes=[
            pltpu.VMEM((2 * BQ, LANES), jnp.float32),
            pltpu.VMEM((2 * BQ, LANES), jnp.float32),
            pltpu.VMEM((2 * BQ, HD), jnp.float32),
        ],
    )
    out = pl.pallas_call(
        kernel,
        grid_spec=grid_spec,
        out_shape=jax.ShapeDtypeStruct((n_q, 2 * BQ, HD), jnp.bfloat16),
    )(new_idx, old_idx, counts, lengths, q2, seg_q, kv_new, kv_new, seg_k, cached, cached)
    return out.reshape(n_q, 2, BQ, HD).transpose(0, 2, 1, 3).reshape(tokens, 2 * HD)


def expert_apply(rows_in, expert_in, expert_out):
    dims_in = rows_in.shape
    flat = rows_in.reshape(-1, dims_in[-1])
    both = jnp.dot(flat, expert_in[0], preferred_element_type=jnp.float32)
    half_units = both.shape[1] // 2
    hidden = (jax.nn.silu(both[:, :half_units]) * both[:, half_units:]).astype(jnp.bfloat16)
    half_out = jnp.dot(hidden, expert_out[0], preferred_element_type=jnp.float32)
    return half_out.reshape(dims_in)


def shards(
    tokens,
    queries,
    new_kv,
    page_pool,
    seg_ids,
    cache_len,
    page_table,
    moves,
    out_weight,
    norm_gain,
    expert_ids,
    gate_weights,
    expert_in,
    expert_out,
):
    n_wide = lax.axis_size("wide")
    n_narrow = lax.axis_size("y") * lax.axis_size("core")
    my_group = lax.axis_index("wide")
    tok_dev, width = tokens.shape
    group_tok = tok_dev * n_narrow
    requests = moves.shape[0]
    page_rows = page_pool.shape[1]
    kv_feat = page_pool.shape[2]
    pages_each = page_pool.shape[0] // requests
    heads_here = QH // n_narrow
    group_size = QH // KVH
    ranks = rank_among_equal(moves)
    offsets = jnp.arange(n_wide, dtype=jnp.int32)
    places = jnp.arange(PAGE_CAP, dtype=jnp.int32)
    slot_hits = (moves[None, None, :] == offsets[:, None, None]) & (
        ranks[None, None, :] == places[None, :, None]
    )
    picked = jnp.sum(slot_hits.astype(jnp.int32) * jnp.arange(requests, dtype=jnp.int32), axis=2)
    filled = jnp.any(slot_hits, axis=2)
    by_dest = (offsets - my_group) % n_wide
    picked = picked[by_dest]
    filled = filled[by_dest]
    blocks = page_pool.reshape(requests, pages_each * page_rows, kv_feat)
    outgoing = jnp.take(blocks, picked.reshape(-1), axis=0).reshape(
        n_wide, PAGE_CAP, pages_each * page_rows, kv_feat
    )
    outgoing = jnp.where(filled[:, :, None, None], outgoing, jnp.zeros((), outgoing.dtype))
    arrived = lax.all_to_all(outgoing, "wide", split_axis=0, concat_axis=0, tiled=True)
    sources = (my_group - moves) % n_wide
    first_page = (sources * PAGE_CAP + ranks) * pages_each
    page_index = (first_page[:, None] + page_table[0]).reshape(-1)
    arrived = arrived.reshape(n_wide * PAGE_CAP * pages_each, page_rows, kv_feat)
    cached = jnp.take(arrived, page_index, axis=0)
    kv_of_dest = jnp.arange(n_narrow, dtype=jnp.int32) * heads_here // group_size
    q_send = queries.reshape(1, tok_dev, n_narrow, heads_here * HD)
    kv_send = jnp.take(new_kv.reshape(tok_dev, KVH, 2 * HD), kv_of_dest, axis=1).reshape(
        1, tok_dev, n_narrow, 2 * HD
    )
    cache_send = jnp.take(
        cached.reshape(requests * pages_each, page_rows, KVH, 2 * HD), kv_of_dest, axis=2
    )
    q_heads, kv_heads, cache_heads = (
        lax.all_to_all(q_send, NARROW, split_axis=2, concat_axis=1, tiled=True),
        lax.all_to_all(kv_send, NARROW, split_axis=2, concat_axis=1, tiled=True),
        lax.all_to_all(cache_send, NARROW, split_axis=2, concat_axis=1, tiled=True),
    )
    q_heads = q_heads.reshape(group_tok, heads_here, HD)
    kv_heads = kv_heads.reshape(group_tok, 2 * HD)
    cache_max = pages_each * page_rows * n_narrow
    cache_heads = cache_heads.reshape(requests * cache_max, 2 * HD)
    key_new = kv_heads[:, :HD]
    value_new = kv_heads[:, HD:]
    key_cached = cache_heads[:, :HD]
    value_cached = cache_heads[:, HD:]
    seg_all = seg_ids[0]
    lengths = cache_len[0]
    attended = slot_attention(
        q_heads.reshape(group_tok, heads_here * HD), kv_heads, cache_heads, seg_all, lengths, cache_max
    ).reshape(n_narrow, tok_dev, heads_here * HD)
    back_home = lax.all_to_all(attended, NARROW, split_axis=0, concat_axis=2, tiled=True)
    mixed = back_home.reshape(tok_dev, QH * HD)
    residual = tokens.astype(jnp.float32) + jnp.dot(
        mixed, out_weight, preferred_element_type=jnp.float32
    )
    scale_row = lax.rsqrt(jnp.mean(residual * residual, axis=-1, keepdims=True) + norm_eps)
    normed = (residual * scale_row * norm_gain).astype(jnp.bfloat16)
    experts = n_wide * n_narrow // 2
    capacity = tok_dev * TOPK * 4 // (3 * experts)
    flat_ids = expert_ids.reshape(-1)
    onehot = (flat_ids[:, None] == jnp.arange(experts, dtype=jnp.int32)[None, :]).astype(jnp.int32)
    before = jnp.cumsum(onehot, axis=0) - onehot
    slot_place = jnp.sum(before * onehot, axis=1)
    slot_of = flat_ids * capacity + slot_place
    token_of = jnp.arange(tok_dev * TOPK, dtype=jnp.int32) // TOPK
    slot_token = jnp.zeros((experts * capacity,), jnp.int32).at[slot_of].set(token_of)
    slot_used = jnp.zeros((experts * capacity,), jnp.bool_).at[slot_of].set(True)
    outgoing_rows = jnp.where(
        slot_used[:, None], jnp.take(normed, slot_token, axis=0), jnp.zeros((), jnp.bfloat16)
    )
    outgoing_rows = outgoing_rows.reshape(experts, capacity, width)
    at_chip = lax.all_to_all(outgoing_rows, CHIPS, split_axis=0, concat_axis=0, tiled=True)
    swap = [(0, 1), (1, 0)]
    partner_rows = lax.ppermute(at_chip, "core", perm=swap)
    own_half = expert_apply(at_chip, expert_in, expert_out)
    own_half, partner_rows = lax.optimization_barrier((own_half, partner_rows))
    partner_half = expert_apply(partner_rows, expert_in, expert_out)
    other_half = lax.ppermute(partner_half, "core", perm=swap)
    summed = (own_half + other_half).astype(jnp.bfloat16)
    returned = lax.all_to_all(summed, CHIPS, split_axis=0, concat_axis=0, tiled=True)
    summed_rows = returned.reshape(experts * capacity, width)
    picked_rows = jnp.take(summed_rows, slot_of, axis=0)
    weighted = picked_rows.astype(jnp.float32) * gate_weights.reshape(-1)[:, None]
    expert_sum = jnp.sum(weighted.reshape(tok_dev, TOPK, width), axis=1)
    return (residual + expert_sum).astype(jnp.bfloat16)


def solution(mesh):
    placed = (
        P(WN, None),
        P(WN, None),
        P(WN, None),
        P("wide", NARROW, None),
        P("wide", None),
        P("wide", None),
        P("wide", None, None),
        P(),
        P(),
        P(),
        P(WN, None),
        P(WN, None),
        P(WN, None, None),
        P(WN, None, None),
    )
    mesh = Mesh(mesh.devices.reshape(mesh.shape["wide"], -1, 2), ("wide", "y", "core"))
    return jax.shard_map(
        shards, mesh=mesh, in_specs=placed, out_specs=P(WN, None), check_vma=False
    )
```

profile of v0, /device:TPU:24, one launch (start us, length us, event | category | flops | bytes accessed | tf_op | source)
XLA Modules:
  0.0 461.8 jit_solution(6806150101692149514)
XLA Ops:
  7.7 4.7 %select_select_fusion.1 = bf16[16,2,64,1024]{3,2,1,0:T(8,128)(2,1)} fusion(bf16[16,2,64,1024]{3,2,1,0:T(8,128)(2,1)} %bitcast.113, pred[16,2]{1,0:T(8,128)(4,1)S(1)} %compare_and_fusion, pred[16,2]{1,0:T(8,128)(4,1)S(1)} %gather_fusion.2), kind=kLoop, calls=%fused_computation.19 | loop fusion | flops 4194304 | bytes 8388672 | tf_op jit(solution)/shard_map/jit(_where)/select_n | solution.py:243
  12.4 8.1 %all-to-all-start.2 = ((bf16[16,2,64,1024]{3,2,1,0:T(8,128)(2,1)}), bf16[16,2,64,1024]{3,2,1,0:T(8,128)(2,1)}, u32[]{:S(2)}, u32[]{:S(2)}) async-start(bf16[16,2,64,1024]{3,2,1,0:T(8,128)(2,1)} %select_select_fusion.1), calls=%async_computation.2 | async-start | bytes 8388608 | tf_op jit(solution)/shard_map/all_to_all | solution.py:244
  22.1 60.2 %all-to-all-done.2 = bf16[16,2,64,1024]{3,2,1,0:T(8,128)(2,1)} async-done(((bf16[16,2,64,1024]{3,2,1,0:T(8,128)(2,1)}), bf16[16,2,64,1024]{3,2,1,0:T(8,128)(2,1)}, u32[]{:S(2)}, u32[]{:S(2)}) %all-to-all-start.2) | async-done | bytes 4194336 | tf_op jit(solution)/shard_map/all_to_all | solution.py:244
  82.3 4.7 %all-to-all-start = ((bf16[1,128,8,256]{1,3,0,2:T(8,128)(2,1)}), bf16[1,128,8,256]{1,3,0,2:T(8,128)(2,1)S(1)}, u32[]{:S(2)}, u32[]{:S(2)}) async-start(bf16[1,128,8,256]{1,3,0,2:T(8,128)(2,1)} %bitcast.123), calls=%async_computation | async-start | bytes 1048576 | tf_op jit(solution)/shard_map/all_to_all | solution.py:259
  94.4 4.6 %gather_fusion.6 = bf16[8,128,8,256]{3,2,1,0:T(8,128)(2,1)} fusion(bf16[128,8,4,256]{3,1,2,0:T(8,128)(2,1)} %broadcast_select_fusion, s32[1024]{0:T(1024)S(1)} %pad_clamp_fusion.4), kind=kCustom, calls=%fused_computation.6 | custom fusion | bytes 8388640 | tf_op jit(solution)/shard_map/jit(_take)/gather | solution.py:255
  103.7 4.9 %all-to-all-start.3 = ((bf16[128,8,8,256]{3,1,0,2:T(8,128)(2,1)}), bf16[128,8,8,256]{3,1,0,2:T(8,128)(2,1)}, u32[]{:S(2)}, u32[]{:S(2)}) async-start(bf16[128,8,8,256]{3,1,0,2:T(8,128)(2,1)} %select_bitcast_fusion), calls=%async_computation.3 | async-start | bytes 8388608 | tf_op jit(solution)/shard_map/all_to_all | solution.py:261
  119.4 36.9 %all-to-all-done.3 = bf16[128,8,8,256]{3,1,0,2:T(8,128)(2,1)} async-done(((bf16[128,8,8,256]{3,1,0,2:T(8,128)(2,1)}), bf16[128,8,8,256]{3,1,0,2:T(8,128)(2,1)}, u32[]{:S(2)}, u32[]{:S(2)}) %all-to-all-start.3) | async-done | bytes 4194336 | tf_op jit(solution)/shard_map/all_to_all | solution.py:261
  156.3 5.5 %all-to-all-start.1 = ((bf16[1,128,8,256]{3,1,0,2:T(8,128)(2,1)}), bf16[1,128,8,256]{3,1,0,2:T(8,128)(2,1)S(1)}, u32[]{:S(2)}, u32[]{:S(2)}) async-start(bf16[1,128,8,256]{3,1,0,2:T(8,128)(2,1)} %fusion.10), calls=%async_computation.1 | async-start | bytes 1048576 | tf_op jit(solution)/shard_map/all_to_all | solution.py:260
  165.0 4.7 %copy.88 = bf16[128,8,8,1,256]{4,2,1,0,3:T(8,128)(2,1)} copy(bf16[128,8,8,1,256]{4,2,0,1,3:T(8,128)(2,1)} %bitcast.29) | data formatting | bytes 8388608 | tf_op jit(solution)/shard_map/all_to_all | solution.py:261
  172.0 56.1 %shard_map.136 = bf16[8,256,128]{2,1,0:T(8,128)(2,1)} custom-call(s32[168]{0:T(256)} %add.329.new_sm, s32[168]{0:T(256)} %add.333.old_sm, s32[16]{0:T(128)} %reshape.541.cnt_sm, s32[16]{0:T(128)} %bitcast.134, bf16[8,256,128]{2,1,0:T(8,128)(2,1)} %bitcast.120, s32[8,256,128]{2,1,0:T(8,128)} %broadcast_in_dim.151.segq_ref, bf16[1024,256]{1,0:T(8,128)(2,1)} %bitcast.116, ...), custom_call_target="tpu_custom_call" | custom-call | tf_op jit(solution)/shard_map/pallas_call | solution.py:183
  230.2 5.5 %all-to-all-start.4 = ((bf16[8,128,256]{1,2,0:T(8,128)(2,1)}), bf16[8,128,256]{1,2,0:T(8,128)(2,1)S(1)}, u32[]{:S(2)}, u32[]{:S(2)}) async-start(bf16[8,128,256]{1,2,0:T(8,128)(2,1)} %bitcast.124), calls=%async_computation.4 | async-start | bytes 1048576 | tf_op jit(solution)/shard_map/all_to_all | solution.py:276
  243.9 4.8 %multiply_reduce_fusion.1 = (f32[128]{0:T(128)S(1)}, f32[128,2048]{1,0:T(8,128)S(1)}) fusion(bf16[128,2048]{0,1:T(8,128)(2,1)S(1)} %bitcast.119, bf16[2048,2048]{1,0:T(8,128)(2,1)} %param.22, bf16[128,2048]{1,0:T(8,128)(2,1)} %param.14), kind=kOutput, calls=%fused_computation.32 | convolution fusion | flops 1074790272 | bytes 10486272 | tf_op jit(solution)/shard_map/dot_general | solution.py:278
  249.8 6.0 %gather_fusion.7 = bf16[1024,2048]{1,0:T(8,128)(2,1)} fusion(bf16[128,2048]{1,0:T(8,128)(2,1)S(1)} %multiply_convert_fusion, s32[1024]{0:T(1024)S(1)} %fusion.20), kind=kCustom, calls=%fused_computation.7 | custom fusion | bytes 8392704 | tf_op jit(solution)/shard_map/jit(_take)/gather | solution.py:294
  258.4 64.7 %all_to_all.75 = bf16[64,16,2048]{2,1,0:T(8,128)(2,1)S(1)} all-to-all(bf16[64,16,2048]{2,1,0:T(8,128)(2,1)S(1)} %select_select_fusion), channel_id=1, replica_groups=mesh['wide'=16,'y'=4,'core'=2] {'wide','y'}, dimensions={0} | all-to-all | bytes 8388608 | tf_op jit(solution)/shard_map/all_to_all | solution.py:297
  323.1 9.2 %fusion.2 = f32[1024,1408]{1,0:T(8,128)S(1)} fusion(bf16[1024,2048]{1,0:T(8,128)(2,1)S(1)} %bitcast.118, bf16[1,2048,1408]{2,1,0:T(8,128)(2,1)} %param.26), kind=kOutput, calls=%fused_computation.15 | convolution fusion | flops 5905580032 | bytes 15728640 | tf_op jit(solution)/shard_map/dot_general | solution.py:194
  333.2 5.6 %fusion.8 = f32[64,16,2048]{2,1,0:T(8,128)} fusion(bf16[64,16,704]{2,1,0:T(8,128)(2,1)S(1)} %bitcast.125, bf16[1,704,2048]{2,1,0:T(8,128)(2,1)S(1)} %copy-done), kind=kOutput, calls=%fused_computation.26 | convolution fusion | flops 2952790016 | bytes 12713984 | tf_op jit(solution)/shard_map/dot_general | solution.py:197
  338.8 6.6 %fusion = f32[1024,1408]{1,0:T(8,128)S(1)} fusion(bf16[1024,2048]{1,0:T(8,128)(2,1)S(1)} %bitcast.137, bf16[1,2048,1408]{2,1,0:T(8,128)(2,1)S(1)} %bitcast.136), kind=kOutput, calls=%fused_computation.13 | convolution fusion | flops 5905580032 | bytes 15728640 | tf_op jit(solution)/shard_map/dot_general | solution.py:194
  350.6 12.9 %collective-permute-done.1 = f32[64,16,2048]{2,1,0:T(8,128)} collective-permute-done((f32[64,16,2048]{2,1,0:T(8,128)S(1)}, f32[64,16,2048]{2,1,0:T(8,128)}, u32[]{:S(2)}, u32[]{:S(2)}) %collective-permute-start.1) | collective-permute-done | bytes 8388640 | tf_op jit(solution)/shard_map/ppermute | solution.py:303
  363.5 9.1 %add_convert_fusion = bf16[64,16,2048]{2,1,0:T(8,128)(2,1)} fusion(f32[64,16,2048]{2,1,0:T(8,128)} %fusion.8, f32[64,16,2048]{2,1,0:T(8,128)} %collective-permute-done.1), kind=kLoop, calls=%fused_computation.12 | loop fusion | flops 4194304 | bytes 20971520 | tf_op jit(solution)/shard_map/convert_element_type | solution.py:304
  372.6 8.4 %all-to-all-start.6 = ((bf16[64,16,2048]{2,1,0:T(8,128)(2,1)}), bf16[64,16,2048]{2,1,0:T(8,128)(2,1)}, u32[]{:S(2)}, u32[]{:S(2)}) async-start(bf16[64,16,2048]{2,1,0:T(8,128)(2,1)} %add_convert_fusion), calls=%async_computation.6 | async-start | bytes 8388608 | tf_op jit(solution)/shard_map/all_to_all | solution.py:305
  381.6 57.1 %all-to-all-done.6 = bf16[64,16,2048]{2,1,0:T(8,128)(2,1)} async-done(((bf16[64,16,2048]{2,1,0:T(8,128)(2,1)}), bf16[64,16,2048]{2,1,0:T(8,128)(2,1)}, u32[]{:S(2)}, u32[]{:S(2)}) %all-to-all-start.6) | async-done | bytes 4194336 | tf_op jit(solution)/shard_map/all_to_all | solution.py:305
  438.6 9.9 %gather_fusion.8 = bf16[768,2048]{1,0:T(8,128)(2,1)} fusion(bf16[1024,2048]{1,0:T(8,128)(2,1)} %bitcast.46, s32[1024]{0:T(1024)S(1)} %pad_clamp_fusion), kind=kCustom, calls=%fused_computation.8 | custom fusion | bytes 6294528 | tf_op jit(solution)/shard_map/jit(_take)/gather | solution.py:307
  448.5 6.3 %gather.59 = bf16[128,6,2048]{2,1,0:T(8,128)(2,1)} reshape(bf16[768,2048]{1,0:T(8,128)(2,1)} %gather_fusion.8) | data formatting | bytes 6291456 | tf_op jit(solution)/shard_map/jit(_take)/gather | solution.py:307
  454.8 6.1 %multiply_reduce_fusion = f32[128,2048]{1,0:T(8,128)S(1)} fusion(f32[128,6]{1,0:T(8,128)S(1)} %copy.96, bf16[128,6,2048]{2,1,0:T(8,128)(2,1)} %gather.59, pred[128,6]{1,0:T(8,128)(4,1)S(1)} %copy.94), kind=kLoop, calls=%fused_computation.11 | loop fusion | flops 6029312 | bytes 4198144 | tf_op jit(solution)/shard_map/reduce_sum | solution.py:309
  (127 shorter events, 58.7 us)
Async XLA Ops:
  0.0 333.2 %copy-start = (bf16[1,704,2048]{2,1,0:T(8,128)(2,1)S(1)}, bf16[1,704,2048]{2,1,0:T(8,128)(2,1)}, u32[]{:S(2)}) copy-start(bf16[1,704,2048]{2,1,0:T(8,128)(2,1)} %param.27) | copy-start | bytes 8650756
  12.4 8.1 %copy-start.12 = (s32[16]{0:T(128)S(1)}, s32[16]{0:T(128)}, u32[]{:S(2)}) copy-start(s32[16]{0:T(128)} %param.21) | copy-start | bytes 196
  12.4 8.4 %copy-start.10 = (s32[1,16,8]{1,2,0:T(8,128)S(1)}, s32[1,16,8]{1,2,0:T(8,128)}, u32[]{:S(2)}) copy-start(s32[1,16,8]{1,2,0:T(8,128)} %param.20) | copy-start | bytes 1540
  12.4 8.6 %copy-start.6 = (bf16[128,2048]{1,0:T(8,128)(2,1)S(1)}, bf16[128,2048]{1,0:T(8,128)(2,1)}, u32[]{:S(2)}) copy-start(bf16[128,2048]{1,0:T(8,128)(2,1)} %param.15) | copy-start | bytes 1572868
  12.4 69.9 %all-to-all-start.2 = ((bf16[16,2,64,1024]{3,2,1,0:T(8,128)(2,1)}), bf16[16,2,64,1024]{3,2,1,0:T(8,128)(2,1)}, u32[]{:S(2)}, u32[]{:S(2)}) async-start(bf16[16,2,64,1024]{3,2,1,0:T(8,128)(2,1)} %select_select_fusion.1), calls=%async_computation.2 | async-start | bytes 8388608 | tf_op jit(solution)/shard_map/all_to_all | solution.py:244
  82.3 21.4 %all-to-all-start = ((bf16[1,128,8,256]{1,3,0,2:T(8,128)(2,1)}), bf16[1,128,8,256]{1,3,0,2:T(8,128)(2,1)S(1)}, u32[]{:S(2)}, u32[]{:S(2)}) async-start(bf16[1,128,8,256]{1,3,0,2:T(8,128)(2,1)} %bitcast.123), calls=%async_computation | async-start | bytes 1048576 | tf_op jit(solution)/shard_map/all_to_all | solution.py:259
  103.7 5.0 %copy-start.7 = (s32[1,1024]{1,0:T(1,128)S(1)}, s32[1,1024]{1,0:T(1,128)}, u32[]{:S(2)}) copy-start(s32[1,1024]{1,0:T(1,128)} %param.18) | copy-start | bytes 12292
  103.7 5.2 %copy-start.8 = (s32[128,6]{0,1:T(8,128)S(1)}, s32[128,6]{0,1:T(8,128)}, u32[]{:S(2)}) copy-start(s32[128,6]{0,1:T(8,128)} %param.24) | copy-start | bytes 9220
  103.7 5.0 %copy-start.4 = (bf16[1,128,8,256]{1,3,0,2:T(8,128)(2,1)}, bf16[1,128,8,256]{1,3,0,2:T(8,128)(2,1)S(1)}, u32[]{:S(2)}) copy-start(bf16[1,128,8,256]{1,3,0,2:T(8,128)(2,1)S(1)} %all-to-all-done) | copy-start | bytes 1572868
  103.7 52.6 %all-to-all-start.3 = ((bf16[128,8,8,256]{3,1,0,2:T(8,128)(2,1)}), bf16[128,8,8,256]{3,1,0,2:T(8,128)(2,1)}, u32[]{:S(2)}, u32[]{:S(2)}) async-start(bf16[128,8,8,256]{3,1,0,2:T(8,128)(2,1)} %select_bitcast_fusion), calls=%async_computation.3 | async-start | bytes 8388608 | tf_op jit(solution)/shard_map/all_to_all | solution.py:261
  116.8 39.5 %copy-start.5 = (s32[64,6,128]{2,0,1:T(8,128)}, s32[64,6,128]{2,0,1:T(8,128)S(1)}, u32[]{:S(2)}) copy-start(s32[64,6,128]{2,0,1:T(8,128)S(1)} %reduce-window.6) | copy-start | bytes 589828
  156.3 13.7 %all-to-all-start.1 = ((bf16[1,128,8,256]{3,1,0,2:T(8,128)(2,1)}), bf16[1,128,8,256]{3,1,0,2:T(8,128)(2,1)S(1)}, u32[]{:S(2)}, u32[]{:S(2)}) async-start(bf16[1,128,8,256]{3,1,0,2:T(8,128)(2,1)} %fusion.10), calls=%async_computation.1 | async-start | bytes 1048576 | tf_op jit(solution)/shard_map/all_to_all | solution.py:260
  170.1 1.9 copy-start.3
  230.2 13.7 %all-to-all-start.4 = ((bf16[8,128,256]{1,2,0:T(8,128)(2,1)}), bf16[8,128,256]{1,2,0:T(8,128)(2,1)S(1)}, u32[]{:S(2)}, u32[]{:S(2)}) async-start(bf16[8,128,256]{1,2,0:T(8,128)(2,1)} %bitcast.124), calls=%async_computation.4 | async-start | bytes 1048576 | tf_op jit(solution)/shard_map/all_to_all | solution.py:276
  243.9 5.8 %copy-start.9 = (f32[2048]{0:T(1024)S(1)}, f32[2048]{0:T(1024)}, u32[]{:S(2)}) copy-start(f32[2048]{0:T(1024)} %param.23) | copy-start | bytes 24580
  248.7 1.0 copy-start.1
  323.1 15.7 %collective-permute-start = (bf16[64,16,2048]{2,1,0:T(8,128)(2,1)S(1)}, bf16[64,16,2048]{2,1,0:T(8,128)(2,1)S(1)}, u32[]{:S(2)}, u32[]{:S(2)}) collective-permute-start(bf16[64,16,2048]{2,1,0:T(8,128)(2,1)S(1)} %all_to_all.75), channel_id=1, source_target_pairs={{0,1},{1,0},{2,3},{3,2},{4,5},{5,4},{6,7},{7,6},{8,9},{9,8},{10,11... | collective-permute-start | bytes 12582920 | tf_op jit(solution)/shard_map/ppermute | solution.py:299
  332.3 6.5 %slice-start = ((s8[5767168]{0:T(1024)(128)(4,1)}), s8[4194304]{0:T(1024)(128)(4,1)S(1)}, s32[]{:S(2)}) async-start(s8[5767168]{0:T(1024)(128)(4,1)} %bitcast.135), calls=%async_computation.7 | async-start | bytes 8388608
  333.2 5.6 %slice-start.1 = ((s8[5767168]{0:T(1024)(128)(4,1)}), s8[1572864]{0:T(1024)(128)(4,1)S(1)}, s32[]{:S(2)}) async-start(s8[5767168]{0:T(1024)(128)(4,1)} %bitcast.135), calls=%async_computation.8 | async-start | bytes 3145728
  349.8 13.7 %collective-permute-start.1 = (f32[64,16,2048]{2,1,0:T(8,128)S(1)}, f32[64,16,2048]{2,1,0:T(8,128)}, u32[]{:S(2)}, u32[]{:S(2)}) collective-permute-start(f32[64,16,2048]{2,1,0:T(8,128)S(1)} %fusion.6), channel_id=1, source_target_pairs={{0,1},{1,0},{2,3},{3,2},{4,5},{5,4},{6,7},{7,6},{8,9},{9,8},{10,11... | collective-permute-start | bytes 25165832 | tf_op jit(solution)/shard_map/ppermute | solution.py:303
  372.6 8.8 %copy-start.11 = (f32[128,6]{0,1:T(8,128)S(1)}, f32[128,6]{0,1:T(8,128)}, u32[]{:S(2)}) copy-start(f32[128,6]{0,1:T(8,128)} %param.25) | copy-start | bytes 9220
  372.6 66.0 %all-to-all-start.6 = ((bf16[64,16,2048]{2,1,0:T(8,128)(2,1)}), bf16[64,16,2048]{2,1,0:T(8,128)(2,1)}, u32[]{:S(2)}, u32[]{:S(2)}) async-start(bf16[64,16,2048]{2,1,0:T(8,128)(2,1)} %add_convert_fusion), calls=%async_computation.6 | async-start | bytes 8388608 | tf_op jit(solution)/shard_map/all_to_all | solution.py:305
  454.8 6.1 %copy-start.2 = (f32[128,2048]{1,0:T(8,128)S(1)}, f32[128,2048]{1,0:T(8,128)}, u32[]{:S(2)}) copy-start(f32[128,2048]{1,0:T(8,128)} %copy-done.1) | copy-start | bytes 3145732
where the time goes:
time: 464 us; the launch traced here: 462 us
  waiting for transfers between devices  168 us (36%)
  blocking collectives  64.7 us (14%)
  local copies, waits for them, and re-layouts  64.1 us (14%)
  Pallas kernels  56.1 us (12%)
  other arithmetic  40.4 us (9%)
  starting transfers between devices  37.9 us (8%)
  matrix products  29.6 us (6%)
    all_to_all x1, blocking collectives, shards(): lax.all_to_all(outgoing_rows, CHIPS, split_axis=0, concat_axis=0, tiled=T...  64.7 us
    all_to_all x1, waiting for transfers between devices, shards(): lax.all_to_all(outgoing, 'wide', split_axis=0, concat_axis=0, tiled=True)  60.2 us
    all_to_all x1, waiting for transfers between devices, shards(): lax.all_to_all(summed, CHIPS, split_axis=0, concat_axis=0, tiled=True)  57.1 us
    pallas_call x1, Pallas kernels, slot_attention(): pl.pallas_call(kernel, grid_spec=grid_spec, out_shape=jax.ShapeDtypeStruc...  56.1 us
    all_to_all x1, waiting for transfers between devices, shards(): lax.all_to_all(cache_send, NARROW, split_axis=2, concat_axis=1, tiled=True)  36.9 us
    gather x2, local copies, waits for them, and re-layouts, shards(): picked_rows = jnp.take(summed_rows, slot_of, axis=0)  16.1 us
    dot_general x2, matrix products, expert_apply(): both = jnp.dot(flat, expert_in[0], preferred_element_type=jnp.float32)  15.8 us
    ppermute x1, waiting for transfers between devices, shards(): other_half = lax.ppermute(partner_half, 'core', perm=swap)  12.9 us
  transfers between devices with their start and end apart: 8, of which 6 were waited for; matrix products, arithmetic and copies ran while one was open for 13% of the time, Pallas kernels for 0%

commit v1 on v0

--- a/solution.py
+++ b/solution.py
@@ -300,8 +300,8 @@
     own_half = expert_apply(at_chip, expert_in, expert_out)
     own_half, partner_rows = lax.optimization_barrier((own_half, partner_rows))
     partner_half = expert_apply(partner_rows, expert_in, expert_out)
-    other_half = lax.ppermute(partner_half, "core", perm=swap)
-    summed = (own_half + other_half).astype(jnp.bfloat16)
+    other_half = lax.ppermute(partner_half.astype(jnp.bfloat16), "core", perm=swap)
+    summed = (own_half + other_half.astype(jnp.float32)).astype(jnp.bfloat16)
     returned = lax.all_to_all(summed, CHIPS, split_axis=0, concat_axis=0, tiled=True)
     summed_rows = returned.reshape(experts * capacity, width)
     picked_rows = jnp.take(summed_rows, slot_of, axis=0)

time: 464 us -> 453 us (0.976)
  waiting for transfers between devices: 168 us -> 162 us
    ppermute x1, waiting for transfers between devices: 12.9 us -> 6.92 us  [shards(): lax.ppermute(partner_half.astype(jnp.bfloat16), 'core', perm=swap)]
where the time goes in v1:
time: 453 us; the launch traced here: 451 us
  waiting for transfers between devices  162 us (36%)
  blocking collectives  64.3 us (14%)
  local copies, waits for them, and re-layouts  64.2 us (14%)
  Pallas kernels  56.5 us (12%)
  starting transfers between devices  37.9 us (8%)
  other arithmetic  37.1 us (8%)
  matrix products  27.6 us (6%)
    all_to_all x1, blocking collectives, shards(): lax.all_to_all(outgoing_rows, CHIPS, split_axis=0, concat_axis=0, tiled=T...  64.3 us
    all_to_all x1, waiting for transfers between devices, shards(): lax.all_to_all(outgoing, 'wide', split_axis=0, concat_axis=0, tiled=True)  60.2 us
    all_to_all x1, waiting for transfers between devices, shards(): lax.all_to_all(summed, CHIPS, split_axis=0, concat_axis=0, tiled=True)  57.1 us
    pallas_call x1, Pallas kernels, slot_attention(): pl.pallas_call(kernel, grid_spec=grid_spec, out_shape=jax.ShapeDtypeStruc...  56.5 us
    all_to_all x1, waiting for transfers between devices, shards(): lax.all_to_all(cache_send, NARROW, split_axis=2, concat_axis=1, tiled=True)  36.9 us
    gather x2, local copies, waits for them, and re-layouts, shards(): picked_rows = jnp.take(summed_rows, slot_of, axis=0)  16.1 us
    dot_general x2, matrix products, expert_apply(): both = jnp.dot(flat, expert_in[0], preferred_element_type=jnp.float32)  15.8 us
  transfers between devices with their start and end apart: 8, of which 6 were waited for; matrix products, arithmetic and copies ran while one was open for 13% of the time, Pallas kernels for 0%

profile of v1, /device:TPU:24, one launch (start us, length us, event | category | flops | bytes accessed | tf_op | source)
XLA Modules:
  0.0 450.6 jit_solution(7212817757666278349)
XLA Ops:
  7.7 4.7 %select_select_fusion.1 = bf16[16,2,64,1024]{3,2,1,0:T(8,128)(2,1)} fusion(bf16[16,2,64,1024]{3,2,1,0:T(8,128)(2,1)} %bitcast.113, pred[16,2]{1,0:T(8,128)(4,1)S(1)} %compare_and_fusion, pred[16,2]{1,0:T(8,128)(4,1)S(1)} %gather_fusion.2), kind=kLoop, calls=%fused_computation.19 | loop fusion | flops 4194304 | bytes 8388672 | tf_op jit(solution)/shard_map/jit(_where)/select_n | solution.py:243
  12.4 8.1 %all-to-all-start.2 = ((bf16[16,2,64,1024]{3,2,1,0:T(8,128)(2,1)}), bf16[16,2,64,1024]{3,2,1,0:T(8,128)(2,1)}, u32[]{:S(2)}, u32[]{:S(2)}) async-start(bf16[16,2,64,1024]{3,2,1,0:T(8,128)(2,1)} %select_select_fusion.1), calls=%async_computation.2 | async-start | bytes 8388608 | tf_op jit(solution)/shard_map/all_to_all | solution.py:244
  22.1 60.2 %all-to-all-done.2 = bf16[16,2,64,1024]{3,2,1,0:T(8,128)(2,1)} async-done(((bf16[16,2,64,1024]{3,2,1,0:T(8,128)(2,1)}), bf16[16,2,64,1024]{3,2,1,0:T(8,128)(2,1)}, u32[]{:S(2)}, u32[]{:S(2)}) %all-to-all-start.2) | async-done | bytes 4194336 | tf_op jit(solution)/shard_map/all_to_all | solution.py:244
  82.3 4.7 %all-to-all-start = ((bf16[1,128,8,256]{1,3,0,2:T(8,128)(2,1)}), bf16[1,128,8,256]{1,3,0,2:T(8,128)(2,1)S(1)}, u32[]{:S(2)}, u32[]{:S(2)}) async-start(bf16[1,128,8,256]{1,3,0,2:T(8,128)(2,1)} %bitcast.123), calls=%async_computation | async-start | bytes 1048576 | tf_op jit(solution)/shard_map/all_to_all | solution.py:259
  94.4 4.6 %gather_fusion.6 = bf16[8,128,8,256]{3,2,1,0:T(8,128)(2,1)} fusion(bf16[128,8,4,256]{3,1,2,0:T(8,128)(2,1)} %broadcast_select_fusion, s32[1024]{0:T(1024)S(1)} %pad_clamp_fusion.4), kind=kCustom, calls=%fused_computation.6 | custom fusion | bytes 8388640 | tf_op jit(solution)/shard_map/jit(_take)/gather | solution.py:255
  99.1 4.6 %select_bitcast_fusion = bf16[128,8,8,256]{3,1,0,2:T(8,128)(2,1)} fusion(bf16[8,128,8,256]{3,2,1,0:T(8,128)(2,1)} %gather_fusion.6, pred[8]{0:T(512)(128)(4,1)S(1)} %compare_and_fusion.4), kind=kLoop, calls=%fused_computation.17 | loop fusion | flops 2097152 | bytes 8388616 | tf_op jit(solution)/shard_map/jit(_take)/select_n | solution.py:255
  103.7 4.9 %all-to-all-start.3 = ((bf16[128,8,8,256]{3,1,0,2:T(8,128)(2,1)}), bf16[128,8,8,256]{3,1,0,2:T(8,128)(2,1)}, u32[]{:S(2)}, u32[]{:S(2)}) async-start(bf16[128,8,8,256]{3,1,0,2:T(8,128)(2,1)} %select_bitcast_fusion), calls=%async_computation.3 | async-start | bytes 8388608 | tf_op jit(solution)/shard_map/all_to_all | solution.py:261
  119.4 36.9 %all-to-all-done.3 = bf16[128,8,8,256]{3,1,0,2:T(8,128)(2,1)} async-done(((bf16[128,8,8,256]{3,1,0,2:T(8,128)(2,1)}), bf16[128,8,8,256]{3,1,0,2:T(8,128)(2,1)}, u32[]{:S(2)}, u32[]{:S(2)}) %all-to-all-start.3) | async-done | bytes 4194336 | tf_op jit(solution)/shard_map/all_to_all | solution.py:261
  156.3 5.5 %all-to-all-start.1 = ((bf16[1,128,8,256]{3,1,0,2:T(8,128)(2,1)}), bf16[1,128,8,256]{3,1,0,2:T(8,128)(2,1)S(1)}, u32[]{:S(2)}, u32[]{:S(2)}) async-start(bf16[1,128,8,256]{3,1,0,2:T(8,128)(2,1)} %fusion.9), calls=%async_computation.1 | async-start | bytes 1048576 | tf_op jit(solution)/shard_map/all_to_all | solution.py:260
  165.0 4.7 %copy.88 = bf16[128,8,8,1,256]{4,2,1,0,3:T(8,128)(2,1)} copy(bf16[128,8,8,1,256]{4,2,0,1,3:T(8,128)(2,1)} %bitcast.29) | data formatting | bytes 8388608 | tf_op jit(solution)/shard_map/all_to_all | solution.py:261
  172.0 56.5 %shard_map.136 = bf16[8,256,128]{2,1,0:T(8,128)(2,1)} custom-call(s32[168]{0:T(256)} %add.329.new_sm, s32[168]{0:T(256)} %add.333.old_sm, s32[16]{0:T(128)} %reshape.541.cnt_sm, s32[16]{0:T(128)} %bitcast.134, bf16[8,256,128]{2,1,0:T(8,128)(2,1)} %bitcast.120, s32[8,256,128]{2,1,0:T(8,128)} %broadcast_in_dim.151.segq_ref, bf16[1024,256]{1,0:T(8,128)(2,1)} %bitcast.116, ...), custom_call_target="tpu_custom_call" | custom-call | tf_op jit(solution)/shard_map/pallas_call | solution.py:183
  230.6 5.5 %all-to-all-start.4 = ((bf16[8,128,256]{1,2,0:T(8,128)(2,1)}), bf16[8,128,256]{1,2,0:T(8,128)(2,1)S(1)}, u32[]{:S(2)}, u32[]{:S(2)}) async-start(bf16[8,128,256]{1,2,0:T(8,128)(2,1)} %bitcast.124), calls=%async_computation.4 | async-start | bytes 1048576 | tf_op jit(solution)/shard_map/all_to_all | solution.py:276
  244.3 4.8 %multiply_reduce_fusion.1 = (f32[128]{0:T(128)S(1)}, f32[128,2048]{1,0:T(8,128)S(1)}) fusion(bf16[128,2048]{0,1:T(8,128)(2,1)S(1)} %bitcast.119, bf16[2048,2048]{1,0:T(8,128)(2,1)} %param.22, bf16[128,2048]{1,0:T(8,128)(2,1)} %param.14), kind=kOutput, calls=%fused_computation.32 | convolution fusion | flops 1074790272 | bytes 10486272 | tf_op jit(solution)/shard_map/dot_general | solution.py:278
  250.4 6.0 %gather_fusion.7 = bf16[1024,2048]{1,0:T(8,128)(2,1)} fusion(bf16[128,2048]{1,0:T(8,128)(2,1)S(1)} %multiply_convert_fusion, s32[1024]{0:T(1024)S(1)} %fusion.19), kind=kCustom, calls=%fused_computation.7 | custom fusion | bytes 8392704 | tf_op jit(solution)/shard_map/jit(_take)/gather | solution.py:294
  259.0 64.3 %all_to_all.75 = bf16[64,16,2048]{2,1,0:T(8,128)(2,1)S(1)} all-to-all(bf16[64,16,2048]{2,1,0:T(8,128)(2,1)S(1)} %select_select_fusion), channel_id=1, replica_groups=mesh['wide'=16,'y'=4,'core'=2] {'wide','y'}, dimensions={0} | all-to-all | bytes 8388608 | tf_op jit(solution)/shard_map/all_to_all | solution.py:297
  323.2 9.2 %fusion.2 = f32[1024,1408]{1,0:T(8,128)S(1)} fusion(bf16[1024,2048]{1,0:T(8,128)(2,1)S(1)} %bitcast.118, bf16[1,2048,1408]{2,1,0:T(8,128)(2,1)} %param.26), kind=kOutput, calls=%fused_computation.15 | convolution fusion | flops 5905580032 | bytes 15728640 | tf_op jit(solution)/shard_map/dot_general | solution.py:194
  336.8 6.6 %fusion = f32[1024,1408]{1,0:T(8,128)S(1)} fusion(bf16[1024,2048]{1,0:T(8,128)(2,1)S(1)} %bitcast.137, bf16[1,2048,1408]{2,1,0:T(8,128)(2,1)S(1)} %bitcast.136), kind=kOutput, calls=%fused_computation.13 | convolution fusion | flops 5905580032 | bytes 15728640 | tf_op jit(solution)/shard_map/dot_general | solution.py:194
  348.7 6.9 %collective-permute-done.1 = bf16[64,16,2048]{2,1,0:T(8,128)(2,1)} collective-permute-done((bf16[64,16,2048]{2,1,0:T(8,128)(2,1)S(1)}, bf16[64,16,2048]{2,1,0:T(8,128)(2,1)}, u32[]{:S(2)}, u32[]{:S(2)}) %collective-permute-start.1) | collective-permute-done | bytes 4194336 | tf_op jit(solution)/shard_map/ppermute | solution.py:303
  355.7 5.9 %add_convert_fusion = bf16[64,16,2048]{2,1,0:T(8,128)(2,1)} fusion(f32[64,16,2048]{2,1,0:T(8,128)S(1)} %fusion.7, bf16[64,16,2048]{2,1,0:T(8,128)(2,1)} %collective-permute-done.1), kind=kLoop, calls=%fused_computation.12 | loop fusion | flops 6291456 | bytes 16777216 | tf_op jit(solution)/shard_map/convert_element_type | solution.py:304
  361.5 8.4 %all-to-all-start.6 = ((bf16[64,16,2048]{2,1,0:T(8,128)(2,1)}), bf16[64,16,2048]{2,1,0:T(8,128)(2,1)}, u32[]{:S(2)}, u32[]{:S(2)}) async-start(bf16[64,16,2048]{2,1,0:T(8,128)(2,1)} %add_convert_fusion), calls=%async_computation.6 | async-start | bytes 8388608 | tf_op jit(solution)/shard_map/all_to_all | solution.py:305
  370.4 57.1 %all-to-all-done.6 = bf16[64,16,2048]{2,1,0:T(8,128)(2,1)} async-done(((bf16[64,16,2048]{2,1,0:T(8,128)(2,1)}), bf16[64,16,2048]{2,1,0:T(8,128)(2,1)}, u32[]{:S(2)}, u32[]{:S(2)}) %all-to-all-start.6) | async-done | bytes 4194336 | tf_op jit(solution)/shard_map/all_to_all | solution.py:305
  427.5 9.9 %gather_fusion.8 = bf16[768,2048]{1,0:T(8,128)(2,1)} fusion(bf16[1024,2048]{1,0:T(8,128)(2,1)} %bitcast.46, s32[1024]{0:T(1024)S(1)} %pad_clamp_fusion), kind=kCustom, calls=%fused_computation.8 | custom fusion | bytes 6294528 | tf_op jit(solution)/shard_map/jit(_take)/gather | solution.py:307
  437.4 6.3 %gather.59 = bf16[128,6,2048]{2,1,0:T(8,128)(2,1)} reshape(bf16[768,2048]{1,0:T(8,128)(2,1)} %gather_fusion.8) | data formatting | bytes 6291456 | tf_op jit(solution)/shard_map/jit(_take)/gather | solution.py:307
  443.6 6.1 %multiply_reduce_fusion = f32[128,2048]{1,0:T(8,128)S(1)} fusion(f32[128,6]{1,0:T(8,128)S(1)} %copy.96, bf16[128,6,2048]{2,1,0:T(8,128)(2,1)} %gather.59, pred[128,6]{1,0:T(8,128)(4,1)S(1)} %copy.94), kind=kLoop, calls=%fused_computation.11 | loop fusion | flops 6029312 | bytes 4198144 | tf_op jit(solution)/shard_map/reduce_sum | solution.py:309
  (127 shorter events, 57.8 us)
Async XLA Ops:
  0.0 333.3 %copy-start = (bf16[1,704,2048]{2,1,0:T(8,128)(2,1)S(1)}, bf16[1,704,2048]{2,1,0:T(8,128)(2,1)}, u32[]{:S(2)}) copy-start(bf16[1,704,2048]{2,1,0:T(8,128)(2,1)} %param.27) | copy-start | bytes 8650756
  12.4 8.1 %copy-start.12 = (s32[16]{0:T(128)S(1)}, s32[16]{0:T(128)}, u32[]{:S(2)}) copy-start(s32[16]{0:T(128)} %param.21) | copy-start | bytes 196
  12.4 8.4 %copy-start.10 = (s32[1,16,8]{1,2,0:T(8,128)S(1)}, s32[1,16,8]{1,2,0:T(8,128)}, u32[]{:S(2)}) copy-start(s32[1,16,8]{1,2,0:T(8,128)} %param.20) | copy-start | bytes 1540
  12.4 8.6 %copy-start.6 = (bf16[128,2048]{1,0:T(8,128)(2,1)S(1)}, bf16[128,2048]{1,0:T(8,128)(2,1)}, u32[]{:S(2)}) copy-start(bf16[128,2048]{1,0:T(8,128)(2,1)} %param.15) | copy-start | bytes 1572868
  12.4 69.9 %all-to-all-start.2 = ((bf16[16,2,64,1024]{3,2,1,0:T(8,128)(2,1)}), bf16[16,2,64,1024]{3,2,1,0:T(8,128)(2,1)}, u32[]{:S(2)}, u32[]{:S(2)}) async-start(bf16[16,2,64,1024]{3,2,1,0:T(8,128)(2,1)} %select_select_fusion.1), calls=%async_computation.2 | async-start | bytes 8388608 | tf_op jit(solution)/shard_map/all_to_all | solution.py:244
  82.3 21.4 %all-to-all-start = ((bf16[1,128,8,256]{1,3,0,2:T(8,128)(2,1)}), bf16[1,128,8,256]{1,3,0,2:T(8,128)(2,1)S(1)}, u32[]{:S(2)}, u32[]{:S(2)}) async-start(bf16[1,128,8,256]{1,3,0,2:T(8,128)(2,1)} %bitcast.123), calls=%async_computation | async-start | bytes 1048576 | tf_op jit(solution)/shard_map/all_to_all | solution.py:259
  103.7 5.0 %copy-start.7 = (s32[1,1024]{1,0:T(1,128)S(1)}, s32[1,1024]{1,0:T(1,128)}, u32[]{:S(2)}) copy-start(s32[1,1024]{1,0:T(1,128)} %param.18) | copy-start | bytes 12292
  103.7 5.2 %copy-start.8 = (s32[128,6]{0,1:T(8,128)S(1)}, s32[128,6]{0,1:T(8,128)}, u32[]{:S(2)}) copy-start(s32[128,6]{0,1:T(8,128)} %param.24) | copy-start | bytes 9220
  103.7 5.0 %copy-start.4 = (bf16[1,128,8,256]{1,3,0,2:T(8,128)(2,1)}, bf16[1,128,8,256]{1,3,0,2:T(8,128)(2,1)S(1)}, u32[]{:S(2)}) copy-start(bf16[1,128,8,256]{1,3,0,2:T(8,128)(2,1)S(1)} %all-to-all-done) | copy-start | bytes 1572868
  103.7 52.6 %all-to-all-start.3 = ((bf16[128,8,8,256]{3,1,0,2:T(8,128)(2,1)}), bf16[128,8,8,256]{3,1,0,2:T(8,128)(2,1)}, u32[]{:S(2)}, u32[]{:S(2)}) async-start(bf16[128,8,8,256]{3,1,0,2:T(8,128)(2,1)} %select_bitcast_fusion), calls=%async_computation.3 | async-start | bytes 8388608 | tf_op jit(solution)/shard_map/all_to_all | solution.py:261
  116.8 39.5 %copy-start.5 = (s32[64,6,128]{2,0,1:T(8,128)}, s32[64,6,128]{2,0,1:T(8,128)S(1)}, u32[]{:S(2)}) copy-start(s32[64,6,128]{2,0,1:T(8,128)S(1)} %reduce-window.6) | copy-start | bytes 589828
  156.3 13.7 %all-to-all-start.1 = ((bf16[1,128,8,256]{3,1,0,2:T(8,128)(2,1)}), bf16[1,128,8,256]{3,1,0,2:T(8,128)(2,1)S(1)}, u32[]{:S(2)}, u32[]{:S(2)}) async-start(bf16[1,128,8,256]{3,1,0,2:T(8,128)(2,1)} %fusion.9), calls=%async_computation.1 | async-start | bytes 1048576 | tf_op jit(solution)/shard_map/all_to_all | solution.py:260
  170.1 1.9 copy-start.3
  230.6 13.7 %all-to-all-start.4 = ((bf16[8,128,256]{1,2,0:T(8,128)(2,1)}), bf16[8,128,256]{1,2,0:T(8,128)(2,1)S(1)}, u32[]{:S(2)}, u32[]{:S(2)}) async-start(bf16[8,128,256]{1,2,0:T(8,128)(2,1)} %bitcast.124), calls=%async_computation.4 | async-start | bytes 1048576 | tf_op jit(solution)/shard_map/all_to_all | solution.py:276
  244.3 5.9 %copy-start.9 = (f32[2048]{0:T(1024)S(1)}, f32[2048]{0:T(1024)}, u32[]{:S(2)}) copy-start(f32[2048]{0:T(1024)} %param.23) | copy-start | bytes 24580
  249.1 1.1 copy-start.1
  323.2 13.5 %collective-permute-start = (bf16[64,16,2048]{2,1,0:T(8,128)(2,1)S(1)}, bf16[64,16,2048]{2,1,0:T(8,128)(2,1)S(1)}, u32[]{:S(2)}, u32[]{:S(2)}) collective-permute-start(bf16[64,16,2048]{2,1,0:T(8,128)(2,1)S(1)} %all_to_all.75), channel_id=1, source_target_pairs={{0,1},{1,0},{2,3},{3,2},{4,5},{5,4},{6,7},{7,6},{8,9},{9,8},{10,11... | collective-permute-start | bytes 12582920 | tf_op jit(solution)/shard_map/ppermute | solution.py:299
  332.4 4.4 slice-start
  333.3 3.5 slice-start.1
  347.9 7.7 %collective-permute-start.1 = (bf16[64,16,2048]{2,1,0:T(8,128)(2,1)S(1)}, bf16[64,16,2048]{2,1,0:T(8,128)(2,1)}, u32[]{:S(2)}, u32[]{:S(2)}) collective-permute-start(bf16[64,16,2048]{2,1,0:T(8,128)(2,1)S(1)} %convolution_convert_fusion), channel_id=1, source_target_pairs={{0,1},{1,0},{2,3},{3,2},{4,5},{5,4},{6,7},{7,6},{8,9},{9,8},{10,11... | collective-permute-start | bytes 12582920 | tf_op jit(solution)/shard_map/ppermute | solution.py:303
  361.5 8.8 %copy-start.11 = (f32[128,6]{0,1:T(8,128)S(1)}, f32[128,6]{0,1:T(8,128)}, u32[]{:S(2)}) copy-start(f32[128,6]{0,1:T(8,128)} %param.25) | copy-start | bytes 9220
  361.5 66.0 %all-to-all-start.6 = ((bf16[64,16,2048]{2,1,0:T(8,128)(2,1)}), bf16[64,16,2048]{2,1,0:T(8,128)(2,1)}, u32[]{:S(2)}, u32[]{:S(2)}) async-start(bf16[64,16,2048]{2,1,0:T(8,128)(2,1)} %add_convert_fusion), calls=%async_computation.6 | async-start | bytes 8388608 | tf_op jit(solution)/shard_map/all_to_all | solution.py:305
  443.6 6.1 %copy-start.2 = (f32[128,2048]{1,0:T(8,128)S(1)}, f32[128,2048]{1,0:T(8,128)}, u32[]{:S(2)}) copy-start(f32[128,2048]{1,0:T(8,128)} %copy-done.1) | copy-start | bytes 3145732

commit v2 on v1

--- a/solution.py
+++ b/solution.py
@@ -304,9 +304,15 @@
     summed = (own_half + other_half.astype(jnp.float32)).astype(jnp.bfloat16)
     returned = lax.all_to_all(summed, CHIPS, split_axis=0, concat_axis=0, tiled=True)
     summed_rows = returned.reshape(experts * capacity, width)
-    picked_rows = jnp.take(summed_rows, slot_of, axis=0)
-    weighted = picked_rows.astype(jnp.float32) * gate_weights.reshape(-1)[:, None]
-    expert_sum = jnp.sum(weighted.reshape(tok_dev, TOPK, width), axis=1)
+    slot_hit = slot_of[:, None] == jnp.arange(experts * capacity, dtype=jnp.int32)[None, :]
+    gate_at = jnp.where(slot_hit, gate_weights.reshape(-1)[:, None], jnp.float32(0.0))
+    gate_at = jnp.sum(gate_at.reshape(tok_dev, TOPK, experts * capacity), axis=1)
+    expert_sum = jnp.dot(
+        gate_at,
+        summed_rows.astype(jnp.float32),
+        precision=lax.Precision.HIGHEST,
+        preferred_element_type=jnp.float32,
+    )
     return (residual + expert_sum).astype(jnp.bfloat16)
 
 

time: 453 us -> 434 us (0.958)
  local copies, waits for them, and re-layouts: 64.2 us -> 49.2 us
  other arithmetic: 37.1 us -> 31.1 us
  matrix products: 27.6 us -> 32.8 us
    gather x2 -> x0, local copies, waits for them, and re-layouts: 16.1 us -> none  [shards(): picked_rows = jnp.take(summed_rows, slot_of, axis=0)]
    reduce_sum x1, other arithmetic: 6.07 us -> 0.43 us  [shards(): jnp.sum(gate_at.reshape(tok_dev, TOPK, experts * capacity), axis=1)]
    dot_general x0 -> x1, matrix products: none -> 5.12 us  [shards(): jnp.dot(gate_at, summed_rows.astype(jnp.float32), precision=lax.Precision...]
  transfers between devices with their start and end apart: 8 -> 8, of which waited for: 6 -> 5; matrix products, arithmetic and copies ran while one was open for 13% -> 14% of each run, Pallas kernels for 0% -> 0%
where the time goes in v2:
time: 434 us; the launch traced here: 431 us
  waiting for transfers between devices  162 us (37%)
  blocking collectives  62.4 us (14%)
  Pallas kernels  56.1 us (13%)
  local copies, waits for them, and re-layouts  49.2 us (11%)
  starting transfers between devices  37.1 us (9%)
  matrix products  32.8 us (8%)
  other arithmetic  31.1 us (7%)
    all_to_all x1, blocking collectives, shards(): lax.all_to_all(outgoing_rows, CHIPS, split_axis=0, concat_axis=0, tiled=T...  62.4 us
    all_to_all x1, waiting for transfers between devices, shards(): lax.all_to_all(outgoing, 'wide', split_axis=0, concat_axis=0, tiled=True)  60.2 us
    all_to_all x1, waiting for transfers between devices, shards(): lax.all_to_all(summed, CHIPS, split_axis=0, concat_axis=0, tiled=True)  57.1 us
    pallas_call x1, Pallas kernels, slot_attention(): pl.pallas_call(kernel, grid_spec=grid_spec, out_shape=jax.ShapeDtypeStruc...  56.1 us
    all_to_all x1, waiting for transfers between devices, shards(): lax.all_to_all(cache_send, NARROW, split_axis=2, concat_axis=1, tiled=True)  36.3 us
    dot_general x2, matrix products, expert_apply(): both = jnp.dot(flat, expert_in[0], preferred_element_type=jnp.float32)  15.8 us
  transfers between devices with their start and end apart: 8, of which 5 were waited for; matrix products, arithmetic and copies ran while one was open for 14% of the time, Pallas kernels for 0%

profile of v2, /device:TPU:24, one launch (start us, length us, event | category | flops | bytes accessed | tf_op | source)
XLA Modules:
  0.0 430.6 jit_solution(16753505200197730936)
XLA Ops:
  3.4 4.3 %gather_fusion.4 = bf16[32,64,1024]{2,1,0:T(8,128)(2,1)} fusion(bf16[16,64,1024]{2,1,0:T(8,128)(2,1)} %bitcast.116, s32[1024]{0:T(1024)S(1)} %pad_clamp_fusion.1), kind=kCustom, calls=%fused_computation.4 | custom fusion | bytes 8388736 | tf_op jit(solution)/shard_map/jit(_take)/gather | solution.py:240
  7.7 4.7 %select_select_fusion.1 = bf16[16,2,64,1024]{3,2,1,0:T(8,128)(2,1)} fusion(bf16[16,2,64,1024]{3,2,1,0:T(8,128)(2,1)} %bitcast.115, pred[16,2]{1,0:T(8,128)(4,1)S(1)} %compare_and_fusion, pred[16,2]{1,0:T(8,128)(4,1)S(1)} %gather_fusion.2), kind=kLoop, calls=%fused_computation.17 | loop fusion | flops 4194304 | bytes 8388672 | tf_op jit(solution)/shard_map/jit(_where)/select_n | solution.py:243
  12.4 8.1 %all-to-all-start.2 = ((bf16[16,2,64,1024]{3,2,1,0:T(8,128)(2,1)}), bf16[16,2,64,1024]{3,2,1,0:T(8,128)(2,1)}, u32[]{:S(2)}, u32[]{:S(2)}) async-start(bf16[16,2,64,1024]{3,2,1,0:T(8,128)(2,1)} %select_select_fusion.1), calls=%async_computation.2 | async-start | bytes 8388608 | tf_op jit(solution)/shard_map/all_to_all | solution.py:244
  22.1 60.2 %all-to-all-done.2 = bf16[16,2,64,1024]{3,2,1,0:T(8,128)(2,1)} async-done(((bf16[16,2,64,1024]{3,2,1,0:T(8,128)(2,1)}), bf16[16,2,64,1024]{3,2,1,0:T(8,128)(2,1)}, u32[]{:S(2)}, u32[]{:S(2)}) %all-to-all-start.2) | async-done | bytes 4194336 | tf_op jit(solution)/shard_map/all_to_all | solution.py:244
  82.3 4.7 %all-to-all-start = ((bf16[1,128,8,256]{1,3,0,2:T(8,128)(2,1)}), bf16[1,128,8,256]{1,3,0,2:T(8,128)(2,1)S(1)}, u32[]{:S(2)}, u32[]{:S(2)}) async-start(bf16[1,128,8,256]{1,3,0,2:T(8,128)(2,1)} %bitcast.125), calls=%async_computation | async-start | bytes 1048576 | tf_op jit(solution)/shard_map/all_to_all | solution.py:259
  87.0 4.2 gather_fusion.5
  94.4 4.6 %gather_fusion.6 = bf16[8,128,8,256]{3,2,1,0:T(8,128)(2,1)} fusion(bf16[128,8,4,256]{3,1,2,0:T(8,128)(2,1)} %broadcast_select_fusion, s32[1024]{0:T(1024)S(1)} %pad_clamp_fusion.3), kind=kCustom, calls=%fused_computation.6 | custom fusion | bytes 8388640 | tf_op jit(solution)/shard_map/jit(_take)/gather | solution.py:255
  99.1 4.6 %select_bitcast_fusion = bf16[128,8,8,256]{3,1,0,2:T(8,128)(2,1)} fusion(bf16[8,128,8,256]{3,2,1,0:T(8,128)(2,1)} %gather_fusion.6, pred[8]{0:T(512)(128)(4,1)S(1)} %compare_and_fusion.3), kind=kLoop, calls=%fused_computation.15 | loop fusion | flops 2097152 | bytes 8388616 | tf_op jit(solution)/shard_map/jit(_take)/select_n | solution.py:255
  103.7 4.9 %all-to-all-start.3 = ((bf16[128,8,8,256]{3,1,0,2:T(8,128)(2,1)}), bf16[128,8,8,256]{3,1,0,2:T(8,128)(2,1)}, u32[]{:S(2)}, u32[]{:S(2)}) async-start(bf16[128,8,8,256]{3,1,0,2:T(8,128)(2,1)} %select_bitcast_fusion), calls=%async_computation.3 | async-start | bytes 8388608 | tf_op jit(solution)/shard_map/all_to_all | solution.py:261
  120.1 36.3 %all-to-all-done.3 = bf16[128,8,8,256]{3,1,0,2:T(8,128)(2,1)} async-done(((bf16[128,8,8,256]{3,1,0,2:T(8,128)(2,1)}), bf16[128,8,8,256]{3,1,0,2:T(8,128)(2,1)}, u32[]{:S(2)}, u32[]{:S(2)}) %all-to-all-start.3) | async-done | bytes 4194336 | tf_op jit(solution)/shard_map/all_to_all | solution.py:261
  156.3 5.5 %all-to-all-start.1 = ((bf16[1,128,8,256]{3,1,0,2:T(8,128)(2,1)}), bf16[1,128,8,256]{3,1,0,2:T(8,128)(2,1)S(1)}, u32[]{:S(2)}, u32[]{:S(2)}) async-start(bf16[1,128,8,256]{3,1,0,2:T(8,128)(2,1)} %fusion.10), calls=%async_computation.1 | async-start | bytes 1048576 | tf_op jit(solution)/shard_map/all_to_all | solution.py:260
  166.4 4.7 %copy.71 = bf16[128,8,8,1,256]{4,2,1,0,3:T(8,128)(2,1)} copy(bf16[128,8,8,1,256]{4,2,0,1,3:T(8,128)(2,1)} %bitcast.29) | data formatting | bytes 8388608 | tf_op jit(solution)/shard_map/all_to_all | solution.py:261
  173.1 56.1 %shard_map.136 = bf16[8,256,128]{2,1,0:T(8,128)(2,1)} custom-call(s32[168]{0:T(256)} %add.316.new_sm, s32[168]{0:T(256)} %add.320.old_sm, s32[16]{0:T(128)} %reshape.539.cnt_sm, s32[16]{0:T(128)} %bitcast.136, bf16[8,256,128]{2,1,0:T(8,128)(2,1)} %bitcast.122, s32[8,256,128]{2,1,0:T(8,128)} %broadcast_in_dim.155.segq_ref, bf16[1024,256]{1,0:T(8,128)(2,1)} %bitcast.118, ...), custom_call_target="tpu_custom_call" | custom-call | tf_op jit(solution)/shard_map/pallas_call | solution.py:183
  231.2 4.8 %all-to-all-start.4 = ((bf16[8,128,256]{1,2,0:T(8,128)(2,1)}), bf16[8,128,256]{1,2,0:T(8,128)(2,1)S(1)}, u32[]{:S(2)}, u32[]{:S(2)}) async-start(bf16[8,128,256]{1,2,0:T(8,128)(2,1)} %bitcast.126), calls=%async_computation.4 | async-start | bytes 1048576 | tf_op jit(solution)/shard_map/all_to_all | solution.py:276
  244.3 4.8 %multiply_reduce_fusion = (f32[128]{0:T(128)S(1)}, f32[128,2048]{1,0:T(8,128)S(1)}) fusion(bf16[128,2048]{0,1:T(8,128)(2,1)S(1)} %bitcast.121, bf16[2048,2048]{1,0:T(8,128)(2,1)} %param.22, bf16[128,2048]{1,0:T(8,128)(2,1)} %param.14), kind=kOutput, calls=%fused_computation.33 | convolution fusion | flops 1074790272 | bytes 10486272 | tf_op jit(solution)/shard_map/dot_general | solution.py:278
  250.3 6.0 %gather_fusion.7 = bf16[1024,2048]{1,0:T(8,128)(2,1)} fusion(bf16[128,2048]{1,0:T(8,128)(2,1)S(1)} %multiply_convert_fusion, s32[1024]{0:T(1024)S(1)} %fusion.20), kind=kCustom, calls=%fused_computation.7 | custom fusion | bytes 8392704 | tf_op jit(solution)/shard_map/jit(_take)/gather | solution.py:294
  258.9 62.4 %all_to_all.75 = bf16[64,16,2048]{2,1,0:T(8,128)(2,1)S(1)} all-to-all(bf16[64,16,2048]{2,1,0:T(8,128)(2,1)S(1)} %select_select_fusion), channel_id=1, replica_groups=mesh['wide'=16,'y'=4,'core'=2] {'wide','y'}, dimensions={0} | all-to-all | bytes 8388608 | tf_op jit(solution)/shard_map/all_to_all | solution.py:297
  321.3 9.2 %fusion.2 = f32[1024,1408]{1,0:T(8,128)S(1)} fusion(bf16[1024,2048]{1,0:T(8,128)(2,1)S(1)} %bitcast.120, bf16[1,2048,1408]{2,1,0:T(8,128)(2,1)} %param.26), kind=kOutput, calls=%fused_computation.13 | convolution fusion | flops 5905580032 | bytes 15728640 | tf_op jit(solution)/shard_map/dot_general | solution.py:194
  334.8 6.6 %fusion = f32[1024,1408]{1,0:T(8,128)S(1)} fusion(bf16[1024,2048]{1,0:T(8,128)(2,1)S(1)} %bitcast.139, bf16[1,2048,1408]{2,1,0:T(8,128)(2,1)S(1)} %bitcast.138), kind=kOutput, calls=%fused_computation.11 | convolution fusion | flops 5905580032 | bytes 15728640 | tf_op jit(solution)/shard_map/dot_general | solution.py:194
  346.8 6.9 %collective-permute-done.1 = bf16[64,16,2048]{2,1,0:T(8,128)(2,1)} collective-permute-done((bf16[64,16,2048]{2,1,0:T(8,128)(2,1)S(1)}, bf16[64,16,2048]{2,1,0:T(8,128)(2,1)}, u32[]{:S(2)}, u32[]{:S(2)}) %collective-permute-start.1) | collective-permute-done | bytes 4194336 | tf_op jit(solution)/shard_map/ppermute | solution.py:303
  353.7 5.9 %add_convert_fusion = bf16[64,16,2048]{2,1,0:T(8,128)(2,1)} fusion(f32[64,16,2048]{2,1,0:T(8,128)S(1)} %fusion.7, bf16[64,16,2048]{2,1,0:T(8,128)(2,1)} %collective-permute-done.1), kind=kLoop, calls=%fused_computation.10 | loop fusion | flops 6291456 | bytes 16777216 | tf_op jit(solution)/shard_map/convert_element_type | solution.py:304
  359.6 8.3 %all-to-all-start.6 = ((bf16[64,16,2048]{2,1,0:T(8,128)(2,1)}), bf16[64,16,2048]{2,1,0:T(8,128)(2,1)}, u32[]{:S(2)}, u32[]{:S(2)}) async-start(bf16[64,16,2048]{2,1,0:T(8,128)(2,1)} %add_convert_fusion), calls=%async_computation.6 | async-start | bytes 8388608 | tf_op jit(solution)/shard_map/all_to_all | solution.py:305
  368.4 57.1 %all-to-all-done.6 = bf16[64,16,2048]{2,1,0:T(8,128)(2,1)} async-done(((bf16[64,16,2048]{2,1,0:T(8,128)(2,1)}), bf16[64,16,2048]{2,1,0:T(8,128)(2,1)}, u32[]{:S(2)}, u32[]{:S(2)}) %all-to-all-start.6) | async-done | bytes 4194336 | tf_op jit(solution)/shard_map/all_to_all | solution.py:305
  425.5 5.1 %fusion.9 = bf16[128,2048]{1,0:T(8,128)(2,1)} fusion(f32[128,2048]{1,0:T(8,128)} %copy-done.1, f32[128,1024]{1,0:T(8,128)S(1)} %select_reduce_fusion, bf16[1024,2048]{1,0:T(8,128)(2,1)} %bitcast.46), kind=kOutput, calls=%fused_computation.30 | convolution fusion | flops 3221749760 | bytes 6291456 | tf_op jit(solution)/shard_map/dot_general | solution.py:310
  (116 shorter events, 50.1 us)
Async XLA Ops:
  0.0 331.4 %copy-start = (bf16[1,704,2048]{2,1,0:T(8,128)(2,1)S(1)}, bf16[1,704,2048]{2,1,0:T(8,128)(2,1)}, u32[]{:S(2)}) copy-start(bf16[1,704,2048]{2,1,0:T(8,128)(2,1)} %param.27) | copy-start | bytes 8650756
  12.4 8.1 %copy-start.10 = (s32[16]{0:T(128)S(1)}, s32[16]{0:T(128)}, u32[]{:S(2)}) copy-start(s32[16]{0:T(128)} %param.21) | copy-start | bytes 196
  12.4 8.4 %copy-start.8 = (s32[1,16,8]{1,2,0:T(8,128)S(1)}, s32[1,16,8]{1,2,0:T(8,128)}, u32[]{:S(2)}) copy-start(s32[1,16,8]{1,2,0:T(8,128)} %param.20) | copy-start | bytes 1540
  12.4 8.6 %copy-start.4 = (bf16[128,2048]{1,0:T(8,128)(2,1)S(1)}, bf16[128,2048]{1,0:T(8,128)(2,1)}, u32[]{:S(2)}) copy-start(bf16[128,2048]{1,0:T(8,128)(2,1)} %param.15) | copy-start | bytes 1572868
  12.4 69.9 %all-to-all-start.2 = ((bf16[16,2,64,1024]{3,2,1,0:T(8,128)(2,1)}), bf16[16,2,64,1024]{3,2,1,0:T(8,128)(2,1)}, u32[]{:S(2)}, u32[]{:S(2)}) async-start(bf16[16,2,64,1024]{3,2,1,0:T(8,128)(2,1)} %select_select_fusion.1), calls=%async_computation.2 | async-start | bytes 8388608 | tf_op jit(solution)/shard_map/all_to_all | solution.py:244
  82.3 21.4 %all-to-all-start = ((bf16[1,128,8,256]{1,3,0,2:T(8,128)(2,1)}), bf16[1,128,8,256]{1,3,0,2:T(8,128)(2,1)S(1)}, u32[]{:S(2)}, u32[]{:S(2)}) async-start(bf16[1,128,8,256]{1,3,0,2:T(8,128)(2,1)} %bitcast.125), calls=%async_computation | async-start | bytes 1048576 | tf_op jit(solution)/shard_map/all_to_all | solution.py:259
  103.7 5.0 %copy-start.5 = (s32[1,1024]{1,0:T(1,128)S(1)}, s32[1,1024]{1,0:T(1,128)}, u32[]{:S(2)}) copy-start(s32[1,1024]{1,0:T(1,128)} %param.18) | copy-start | bytes 12292
  103.7 5.2 %copy-start.9 = (s32[128,6]{0,1:T(8,128)S(1)}, s32[128,6]{0,1:T(8,128)}, u32[]{:S(2)}) copy-start(s32[128,6]{0,1:T(8,128)} %param.24) | copy-start | bytes 9220
  103.7 5.0 %copy-start.3 = (bf16[1,128,8,256]{1,3,0,2:T(8,128)(2,1)}, bf16[1,128,8,256]{1,3,0,2:T(8,128)(2,1)S(1)}, u32[]{:S(2)}) copy-start(bf16[1,128,8,256]{1,3,0,2:T(8,128)(2,1)S(1)} %all-to-all-done) | copy-start | bytes 1572868
  103.7 52.6 %all-to-all-start.3 = ((bf16[128,8,8,256]{3,1,0,2:T(8,128)(2,1)}), bf16[128,8,8,256]{3,1,0,2:T(8,128)(2,1)}, u32[]{:S(2)}, u32[]{:S(2)}) async-start(bf16[128,8,8,256]{3,1,0,2:T(8,128)(2,1)} %select_bitcast_fusion), calls=%async_computation.3 | async-start | bytes 8388608 | tf_op jit(solution)/shard_map/all_to_all | solution.py:261
  156.3 14.8 %all-to-all-start.1 = ((bf16[1,128,8,256]{3,1,0,2:T(8,128)(2,1)}), bf16[1,128,8,256]{3,1,0,2:T(8,128)(2,1)S(1)}, u32[]{:S(2)}, u32[]{:S(2)}) async-start(bf16[1,128,8,256]{3,1,0,2:T(8,128)(2,1)} %fusion.10), calls=%async_computation.1 | async-start | bytes 1048576 | tf_op jit(solution)/shard_map/all_to_all | solution.py:260
  171.2 1.9 copy-start.2
  231.2 13.0 %all-to-all-start.4 = ((bf16[8,128,256]{1,2,0:T(8,128)(2,1)}), bf16[8,128,256]{1,2,0:T(8,128)(2,1)S(1)}, u32[]{:S(2)}, u32[]{:S(2)}) async-start(bf16[8,128,256]{1,2,0:T(8,128)(2,1)} %bitcast.126), calls=%async_computation.4 | async-start | bytes 1048576 | tf_op jit(solution)/shard_map/all_to_all | solution.py:276
  244.3 5.9 %copy-start.6 = (f32[2048]{0:T(1024)S(1)}, f32[2048]{0:T(1024)}, u32[]{:S(2)}) copy-start(f32[2048]{0:T(1024)} %param.23) | copy-start | bytes 24580
  249.1 1.1 copy-start.1
  321.3 13.5 %collective-permute-start = (bf16[64,16,2048]{2,1,0:T(8,128)(2,1)S(1)}, bf16[64,16,2048]{2,1,0:T(8,128)(2,1)S(1)}, u32[]{:S(2)}, u32[]{:S(2)}) collective-permute-start(bf16[64,16,2048]{2,1,0:T(8,128)(2,1)S(1)} %all_to_all.75), channel_id=1, source_target_pairs={{0,1},{1,0},{2,3},{3,2},{4,5},{5,4},{6,7},{7,6},{8,9},{9,8},{10,11... | collective-permute-start | bytes 12582920 | tf_op jit(solution)/shard_map/ppermute | solution.py:299
  330.5 4.4 %slice-start = ((s8[5767168]{0:T(1024)(128)(4,1)}), s8[4194304]{0:T(1024)(128)(4,1)S(1)}, s32[]{:S(2)}) async-start(s8[5767168]{0:T(1024)(128)(4,1)} %bitcast.137), calls=%async_computation.7 | async-start | bytes 8388608
  331.4 3.5 slice-start.1
  346.0 7.7 %collective-permute-start.1 = (bf16[64,16,2048]{2,1,0:T(8,128)(2,1)S(1)}, bf16[64,16,2048]{2,1,0:T(8,128)(2,1)}, u32[]{:S(2)}, u32[]{:S(2)}) collective-permute-start(bf16[64,16,2048]{2,1,0:T(8,128)(2,1)S(1)} %convolution_convert_fusion), channel_id=1, source_target_pairs={{0,1},{1,0},{2,3},{3,2},{4,5},{5,4},{6,7},{7,6},{8,9},{9,8},{10,11... | collective-permute-start | bytes 12582920 | tf_op jit(solution)/shard_map/ppermute | solution.py:303
  359.6 8.4 %copy-start.7 = (f32[128,6]{0,1:T(8,128)S(1)}, f32[128,6]{0,1:T(8,128)}, u32[]{:S(2)}) copy-start(f32[128,6]{0,1:T(8,128)} %param.25) | copy-start | bytes 9220
  359.6 65.9 %all-to-all-start.6 = ((bf16[64,16,2048]{2,1,0:T(8,128)(2,1)}), bf16[64,16,2048]{2,1,0:T(8,128)(2,1)}, u32[]{:S(2)}, u32[]{:S(2)}) async-start(bf16[64,16,2048]{2,1,0:T(8,128)(2,1)} %add_convert_fusion), calls=%async_computation.6 | async-start | bytes 8388608 | tf_op jit(solution)/shard_map/all_to_all | solution.py:305

commit v3 on v2

--- a/solution.py
+++ b/solution.py
@@ -287,12 +287,9 @@
     before = jnp.cumsum(onehot, axis=0) - onehot
     slot_place = jnp.sum(before * onehot, axis=1)
     slot_of = flat_ids * capacity + slot_place
-    token_of = jnp.arange(tok_dev * TOPK, dtype=jnp.int32) // TOPK
-    slot_token = jnp.zeros((experts * capacity,), jnp.int32).at[slot_of].set(token_of)
-    slot_used = jnp.zeros((experts * capacity,), jnp.bool_).at[slot_of].set(True)
-    outgoing_rows = jnp.where(
-        slot_used[:, None], jnp.take(normed, slot_token, axis=0), jnp.zeros((), jnp.bfloat16)
-    )
+    slot_hit = slot_of[None, :] == jnp.arange(experts * capacity, dtype=jnp.int32)[:, None]
+    pick = jnp.any(slot_hit.reshape(experts * capacity, tok_dev, TOPK), axis=2).astype(jnp.bfloat16)
+    outgoing_rows = jnp.dot(pick, normed, preferred_element_type=jnp.float32).astype(jnp.bfloat16)
     outgoing_rows = outgoing_rows.reshape(experts, capacity, width)
     at_chip = lax.all_to_all(outgoing_rows, CHIPS, split_axis=0, concat_axis=0, tiled=True)
     swap = [(0, 1), (1, 0)]
@@ -304,8 +301,7 @@
     summed = (own_half + other_half.astype(jnp.float32)).astype(jnp.bfloat16)
     returned = lax.all_to_all(summed, CHIPS, split_axis=0, concat_axis=0, tiled=True)
     summed_rows = returned.reshape(experts * capacity, width)
-    slot_hit = slot_of[:, None] == jnp.arange(experts * capacity, dtype=jnp.int32)[None, :]
-    gate_at = jnp.where(slot_hit, gate_weights.reshape(-1)[:, None], jnp.float32(0.0))
+    gate_at = jnp.where(slot_hit.T, gate_weights.reshape(-1)[:, None], jnp.float32(0.0))
     gate_at = jnp.sum(gate_at.reshape(tok_dev, TOPK, experts * capacity), axis=1)
     expert_sum = jnp.dot(
         gate_at,

time: 434 us -> 428 us (0.986)
  local copies, waits for them, and re-layouts: 49.2 us -> 34.2 us
  waiting for transfers between devices: 162 us -> 170 us
    scatter x2 -> x0, local copies, waits for them, and re-layouts: 6.94 us -> none  [the longest x1 3.56 us: shards(): jnp.zeros((experts * capacity,), jnp.bool_).at[slot_of].set(True)]
    gather x1 -> x0, local copies, waits for them, and re-layouts: 6.02 us -> none  [shards(): jnp.take(normed, slot_token, axis=0)]
    all_to_all x1, waiting for transfers between devices: 1.07 us -> 6.46 us  [shards(): lax.all_to_all(attended, NARROW, split_axis=0, concat_axis=2, tiled=True)]
  transfers between devices with their start and end apart: 8 -> 8, of which waited for: 5 -> 5; matrix products, arithmetic and copies ran while one was open for 14% -> 12% of each run, Pallas kernels for 0% -> 0%
where the time goes in v3:
time: 428 us; the launch traced here: 426 us
  waiting for transfers between devices  170 us (40%)
  blocking collectives  64.7 us (15%)
  Pallas kernels  56.1 us (13%)
  starting transfers between devices  36.9 us (9%)
  local copies, waits for them, and re-layouts  34.2 us (8%)
  matrix products  31.8 us (7%)
  other arithmetic  31.5 us (7%)
    all_to_all x1, blocking collectives, shards(): lax.all_to_all(outgoing_rows, CHIPS, split_axis=0, concat_axis=0, tiled=T...  64.7 us
    all_to_all x1, waiting for transfers between devices, shards(): lax.all_to_all(outgoing, 'wide', split_axis=0, concat_axis=0, tiled=True)  60.2 us
    all_to_all x1, waiting for transfers between devices, shards(): lax.all_to_all(summed, CHIPS, split_axis=0, concat_axis=0, tiled=True)  57.2 us
    pallas_call x1, Pallas kernels, slot_attention(): pl.pallas_call(kernel, grid_spec=grid_spec, out_shape=jax.ShapeDtypeStruc...  56.1 us
    all_to_all x1, waiting for transfers between devices, shards(): lax.all_to_all(cache_send, NARROW, split_axis=2, concat_axis=1, tiled=True)  39.4 us
    dot_general x2, matrix products, expert_apply(): both = jnp.dot(flat, expert_in[0], preferred_element_type=jnp.float32)  13.3 us
  transfers between devices with their start and end apart: 8, of which 5 were waited for; matrix products, arithmetic and copies ran while one was open for 12% of the time, Pallas kernels for 0%

profile of v3, /device:TPU:24, one launch (start us, length us, event | category | flops | bytes accessed | tf_op | source)
XLA Modules:
  0.0 425.7 jit_solution(874460215709126960)
XLA Ops:
  3.4 4.3 %gather_fusion.4 = bf16[32,64,1024]{2,1,0:T(8,128)(2,1)} fusion(bf16[16,64,1024]{2,1,0:T(8,128)(2,1)} %bitcast.117, s32[1024]{0:T(1024)S(1)} %pad_clamp_fusion.1), kind=kCustom, calls=%fused_computation.4 | custom fusion | bytes 8388736 | tf_op jit(solution)/shard_map/jit(_take)/gather | solution.py:240
  7.7 4.7 %select_select_fusion = bf16[16,2,64,1024]{3,2,1,0:T(8,128)(2,1)} fusion(bf16[16,2,64,1024]{3,2,1,0:T(8,128)(2,1)} %bitcast.116, pred[16,2]{1,0:T(8,128)(4,1)S(1)} %compare_and_fusion, pred[16,2]{1,0:T(8,128)(4,1)S(1)} %gather_fusion.2), kind=kLoop, calls=%fused_computation.13 | loop fusion | flops 4194304 | bytes 8388672 | tf_op jit(solution)/shard_map/jit(_where)/select_n | solution.py:243
  12.4 8.1 %all-to-all-start.2 = ((bf16[16,2,64,1024]{3,2,1,0:T(8,128)(2,1)}), bf16[16,2,64,1024]{3,2,1,0:T(8,128)(2,1)}, u32[]{:S(2)}, u32[]{:S(2)}) async-start(bf16[16,2,64,1024]{3,2,1,0:T(8,128)(2,1)} %select_select_fusion), calls=%async_computation.2 | async-start | bytes 8388608 | tf_op jit(solution)/shard_map/all_to_all | solution.py:244
  22.1 60.2 %all-to-all-done.2 = bf16[16,2,64,1024]{3,2,1,0:T(8,128)(2,1)} async-done(((bf16[16,2,64,1024]{3,2,1,0:T(8,128)(2,1)}), bf16[16,2,64,1024]{3,2,1,0:T(8,128)(2,1)}, u32[]{:S(2)}, u32[]{:S(2)}) %all-to-all-start.2) | async-done | bytes 4194336 | tf_op jit(solution)/shard_map/all_to_all | solution.py:244
  82.3 4.7 %all-to-all-start = ((bf16[1,128,8,256]{1,3,0,2:T(8,128)(2,1)}), bf16[1,128,8,256]{1,3,0,2:T(8,128)(2,1)S(1)}, u32[]{:S(2)}, u32[]{:S(2)}) async-start(bf16[1,128,8,256]{1,3,0,2:T(8,128)(2,1)} %bitcast.126), calls=%async_computation | async-start | bytes 1048576 | tf_op jit(solution)/shard_map/all_to_all | solution.py:259
  94.4 4.6 %gather_fusion.6 = bf16[8,128,8,256]{3,2,1,0:T(8,128)(2,1)} fusion(bf16[128,8,4,256]{3,1,2,0:T(8,128)(2,1)} %broadcast_select_fusion, s32[1024]{0:T(1024)S(1)} %pad_clamp_fusion.3), kind=kCustom, calls=%fused_computation.6 | custom fusion | bytes 8388640 | tf_op jit(solution)/shard_map/jit(_take)/gather | solution.py:255
  99.1 4.6 %select_bitcast_fusion = bf16[128,8,8,256]{3,1,0,2:T(8,128)(2,1)} fusion(bf16[8,128,8,256]{3,2,1,0:T(8,128)(2,1)} %gather_fusion.6, pred[8]{0:T(512)(128)(4,1)S(1)} %compare_and_fusion.2), kind=kLoop, calls=%fused_computation.12 | loop fusion | flops 2097152 | bytes 8388616 | tf_op jit(solution)/shard_map/jit(_take)/select_n | solution.py:255
  103.7 4.9 %all-to-all-start.3 = ((bf16[128,8,8,256]{3,1,0,2:T(8,128)(2,1)}), bf16[128,8,8,256]{3,1,0,2:T(8,128)(2,1)}, u32[]{:S(2)}, u32[]{:S(2)}) async-start(bf16[128,8,8,256]{3,1,0,2:T(8,128)(2,1)} %select_bitcast_fusion), calls=%async_computation.3 | async-start | bytes 8388608 | tf_op jit(solution)/shard_map/all_to_all | solution.py:261
  116.9 39.4 %all-to-all-done.3 = bf16[128,8,8,256]{3,1,0,2:T(8,128)(2,1)} async-done(((bf16[128,8,8,256]{3,1,0,2:T(8,128)(2,1)}), bf16[128,8,8,256]{3,1,0,2:T(8,128)(2,1)}, u32[]{:S(2)}, u32[]{:S(2)}) %all-to-all-start.3) | async-done | bytes 4194336 | tf_op jit(solution)/shard_map/all_to_all | solution.py:261
  156.3 5.5 %all-to-all-start.1 = ((bf16[1,128,8,256]{3,1,0,2:T(8,128)(2,1)}), bf16[1,128,8,256]{3,1,0,2:T(8,128)(2,1)S(1)}, u32[]{:S(2)}, u32[]{:S(2)}) async-start(bf16[1,128,8,256]{3,1,0,2:T(8,128)(2,1)} %fusion.11), calls=%async_computation.1 | async-start | bytes 1048576 | tf_op jit(solution)/shard_map/all_to_all | solution.py:260
  162.5 4.4 %reduce-window.6 = s32[64,6,128]{2,0,1:T(8,128)} reduce-window(s32[64,6,128]{2,0,1:T(8,128)} %fusion.17, s32[]{:T(128)} %constant.130.clone.1), window={size=1x1x128 pad=0_0x0_0x127_0}, to_apply=%region_4.5 | reduce-window | flops 6242304 | bytes 393220 | tf_op jit(solution)/shard_map/reduce-window
  170.2 4.7 %copy.94 = bf16[128,8,8,1,256]{4,2,1,0,3:T(8,128)(2,1)} copy(bf16[128,8,8,1,256]{4,2,0,1,3:T(8,128)(2,1)} %bitcast.29) | data formatting | bytes 8388608 | tf_op jit(solution)/shard_map/all_to_all | solution.py:261
  176.9 56.1 %shard_map.136 = bf16[8,256,128]{2,1,0:T(8,128)(2,1)} custom-call(s32[168]{0:T(256)} %add.288.new_sm, s32[168]{0:T(256)} %add.292.old_sm, s32[16]{0:T(128)} %reshape.508.cnt_sm, s32[16]{0:T(128)} %bitcast.137, bf16[8,256,128]{2,1,0:T(8,128)(2,1)} %bitcast.123, s32[8,256,128]{2,1,0:T(8,128)} %broadcast_in_dim.115.segq_ref, bf16[1024,256]{1,0:T(8,128)(2,1)} %bitcast.119, ...), custom_call_target="tpu_custom_call" | custom-call | tf_op jit(solution)/shard_map/pallas_call | solution.py:183
  235.1 4.8 %all-to-all-start.4 = ((bf16[8,128,256]{1,2,0:T(8,128)(2,1)}), bf16[8,128,256]{1,2,0:T(8,128)(2,1)S(1)}, u32[]{:S(2)}, u32[]{:S(2)}) async-start(bf16[8,128,256]{1,2,0:T(8,128)(2,1)} %bitcast.127), calls=%async_computation.4 | async-start | bytes 1048576 | tf_op jit(solution)/shard_map/all_to_all | solution.py:276
  241.7 6.5 %all-to-all-done.4 = bf16[8,128,256]{1,2,0:T(8,128)(2,1)S(1)} async-done(((bf16[8,128,256]{1,2,0:T(8,128)(2,1)}), bf16[8,128,256]{1,2,0:T(8,128)(2,1)S(1)}, u32[]{:S(2)}, u32[]{:S(2)}) %all-to-all-start.4) | async-done | bytes 524320 | tf_op jit(solution)/shard_map/all_to_all | solution.py:276
  248.1 4.8 %multiply_reduce_fusion = (f32[128]{0:T(128)S(1)}, f32[128,2048]{1,0:T(8,128)S(1)}) fusion(bf16[128,2048]{0,1:T(8,128)(2,1)S(1)} %bitcast.122, bf16[2048,2048]{1,0:T(8,128)(2,1)} %param.22, bf16[128,2048]{1,0:T(8,128)(2,1)} %param.14), kind=kOutput, calls=%fused_computation.32 | convolution fusion | flops 1074790272 | bytes 10486272 | tf_op jit(solution)/shard_map/dot_general | solution.py:278
  254.3 64.7 %all_to_all.75 = bf16[64,16,2048]{2,1,0:T(8,128)(2,1)S(1)} all-to-all(bf16[64,16,2048]{2,1,0:T(8,128)(2,1)S(1)} %bitcast.115), channel_id=1, replica_groups=mesh['wide'=16,'y'=4,'core'=2] {'wide','y'}, dimensions={0} | all-to-all | bytes 8388608 | tf_op jit(solution)/shard_map/all_to_all | solution.py:294
  319.0 6.6 %fusion.2 = f32[1024,1408]{1,0:T(8,128)S(1)} fusion(bf16[1024,2048]{1,0:T(8,128)(2,1)S(1)} %bitcast.121, bf16[1,2048,1408]{2,1,0:T(8,128)(2,1)S(1)} %bitcast.139), kind=kOutput, calls=%fused_computation.10 | convolution fusion | flops 5905580032 | bytes 15728640 | tf_op jit(solution)/shard_map/dot_general | solution.py:194
  330.0 6.6 %fusion = f32[1024,1408]{1,0:T(8,128)S(1)} fusion(bf16[1024,2048]{1,0:T(8,128)(2,1)S(1)} %bitcast.140, bf16[1,2048,1408]{2,1,0:T(8,128)(2,1)S(1)} %bitcast.139), kind=kOutput, calls=%fused_computation.8 | convolution fusion | flops 5905580032 | bytes 15728640 | tf_op jit(solution)/shard_map/dot_general | solution.py:194
  341.9 6.9 %collective-permute-done.1 = bf16[64,16,2048]{2,1,0:T(8,128)(2,1)} collective-permute-done((bf16[64,16,2048]{2,1,0:T(8,128)(2,1)S(1)}, bf16[64,16,2048]{2,1,0:T(8,128)(2,1)}, u32[]{:S(2)}, u32[]{:S(2)}) %collective-permute-start.1) | collective-permute-done | bytes 4194336 | tf_op jit(solution)/shard_map/ppermute | solution.py:300
  348.9 5.9 %add_convert_fusion = bf16[64,16,2048]{2,1,0:T(8,128)(2,1)} fusion(f32[64,16,2048]{2,1,0:T(8,128)S(1)} %fusion.8, bf16[64,16,2048]{2,1,0:T(8,128)(2,1)} %collective-permute-done.1), kind=kLoop, calls=%fused_computation.7 | loop fusion | flops 6291456 | bytes 16777216 | tf_op jit(solution)/shard_map/convert_element_type | solution.py:301
  354.7 8.3 %all-to-all-start.6 = ((bf16[64,16,2048]{2,1,0:T(8,128)(2,1)}), bf16[64,16,2048]{2,1,0:T(8,128)(2,1)}, u32[]{:S(2)}, u32[]{:S(2)}) async-start(bf16[64,16,2048]{2,1,0:T(8,128)(2,1)} %add_convert_fusion), calls=%async_computation.6 | async-start | bytes 8388608 | tf_op jit(solution)/shard_map/all_to_all | solution.py:302
  363.4 57.2 %all-to-all-done.6 = bf16[64,16,2048]{2,1,0:T(8,128)(2,1)} async-done(((bf16[64,16,2048]{2,1,0:T(8,128)(2,1)}), bf16[64,16,2048]{2,1,0:T(8,128)(2,1)}, u32[]{:S(2)}, u32[]{:S(2)}) %all-to-all-start.6) | async-done | bytes 4194336 | tf_op jit(solution)/shard_map/all_to_all | solution.py:302
  420.6 5.1 %fusion.10 = bf16[128,2048]{1,0:T(8,128)(2,1)} fusion(f32[128,2048]{1,0:T(8,128)} %copy-done.1, f32[128,1024]{1,0:T(8,128)S(1)} %select_reduce_fusion, bf16[1024,2048]{1,0:T(8,128)(2,1)} %bitcast.46), kind=kOutput, calls=%fused_computation.29 | convolution fusion | flops 3221749760 | bytes 6291456 | tf_op jit(solution)/shard_map/dot_general | solution.py:306
  (105 shorter events, 41.7 us)
Async XLA Ops:
  0.0 326.5 %copy-start = (bf16[1,704,2048]{2,1,0:T(8,128)(2,1)S(1)}, bf16[1,704,2048]{2,1,0:T(8,128)(2,1)}, u32[]{:S(2)}) copy-start(bf16[1,704,2048]{2,1,0:T(8,128)(2,1)} %param.27) | copy-start | bytes 8650756
  12.4 8.1 %copy-start.10 = (s32[16]{0:T(128)S(1)}, s32[16]{0:T(128)}, u32[]{:S(2)}) copy-start(s32[16]{0:T(128)} %param.21) | copy-start | bytes 196
  12.4 8.4 %copy-start.9 = (s32[1,16,8]{1,2,0:T(8,128)S(1)}, s32[1,16,8]{1,2,0:T(8,128)}, u32[]{:S(2)}) copy-start(s32[1,16,8]{1,2,0:T(8,128)} %param.20) | copy-start | bytes 1540
  12.4 8.6 %copy-start.4 = (bf16[128,2048]{1,0:T(8,128)(2,1)S(1)}, bf16[128,2048]{1,0:T(8,128)(2,1)}, u32[]{:S(2)}) copy-start(bf16[128,2048]{1,0:T(8,128)(2,1)} %param.15) | copy-start | bytes 1572868
  12.4 69.9 %all-to-all-start.2 = ((bf16[16,2,64,1024]{3,2,1,0:T(8,128)(2,1)}), bf16[16,2,64,1024]{3,2,1,0:T(8,128)(2,1)}, u32[]{:S(2)}, u32[]{:S(2)}) async-start(bf16[16,2,64,1024]{3,2,1,0:T(8,128)(2,1)} %select_select_fusion), calls=%async_computation.2 | async-start | bytes 8388608 | tf_op jit(solution)/shard_map/all_to_all | solution.py:244
  82.3 21.3 %all-to-all-start = ((bf16[1,128,8,256]{1,3,0,2:T(8,128)(2,1)}), bf16[1,128,8,256]{1,3,0,2:T(8,128)(2,1)S(1)}, u32[]{:S(2)}, u32[]{:S(2)}) async-start(bf16[1,128,8,256]{1,3,0,2:T(8,128)(2,1)} %bitcast.126), calls=%async_computation | async-start | bytes 1048576 | tf_op jit(solution)/shard_map/all_to_all | solution.py:259
  103.7 5.0 %copy-start.5 = (s32[1,1024]{1,0:T(1,128)S(1)}, s32[1,1024]{1,0:T(1,128)}, u32[]{:S(2)}) copy-start(s32[1,1024]{1,0:T(1,128)} %param.18) | copy-start | bytes 12292
  103.7 5.2 %copy-start.6 = (s32[128,6]{0,1:T(8,128)S(1)}, s32[128,6]{0,1:T(8,128)}, u32[]{:S(2)}) copy-start(s32[128,6]{0,1:T(8,128)} %param.24) | copy-start | bytes 9220
  103.7 5.0 %copy-start.3 = (bf16[1,128,8,256]{1,3,0,2:T(8,128)(2,1)}, bf16[1,128,8,256]{1,3,0,2:T(8,128)(2,1)S(1)}, u32[]{:S(2)}) copy-start(bf16[1,128,8,256]{1,3,0,2:T(8,128)(2,1)S(1)} %all-to-all-done) | copy-start | bytes 1572868
  103.7 52.6 %all-to-all-start.3 = ((bf16[128,8,8,256]{3,1,0,2:T(8,128)(2,1)}), bf16[128,8,8,256]{3,1,0,2:T(8,128)(2,1)}, u32[]{:S(2)}, u32[]{:S(2)}) async-start(bf16[128,8,8,256]{3,1,0,2:T(8,128)(2,1)} %select_bitcast_fusion), calls=%async_computation.3 | async-start | bytes 8388608 | tf_op jit(solution)/shard_map/all_to_all | solution.py:261
  156.3 18.6 %all-to-all-start.1 = ((bf16[1,128,8,256]{3,1,0,2:T(8,128)(2,1)}), bf16[1,128,8,256]{3,1,0,2:T(8,128)(2,1)S(1)}, u32[]{:S(2)}, u32[]{:S(2)}) async-start(bf16[1,128,8,256]{3,1,0,2:T(8,128)(2,1)} %fusion.11), calls=%async_computation.1 | async-start | bytes 1048576 | tf_op jit(solution)/shard_map/all_to_all | solution.py:260
  175.0 1.9 copy-start.2
  235.1 13.0 %all-to-all-start.4 = ((bf16[8,128,256]{1,2,0:T(8,128)(2,1)}), bf16[8,128,256]{1,2,0:T(8,128)(2,1)S(1)}, u32[]{:S(2)}, u32[]{:S(2)}) async-start(bf16[8,128,256]{1,2,0:T(8,128)(2,1)} %bitcast.127), calls=%async_computation.4 | async-start | bytes 1048576 | tf_op jit(solution)/shard_map/all_to_all | solution.py:276
  248.1 4.8 %copy-start.7 = (f32[2048]{0:T(1024)S(1)}, f32[2048]{0:T(1024)}, u32[]{:S(2)}) copy-start(f32[2048]{0:T(1024)} %param.23) | copy-start | bytes 24580
  252.9 66.1 %copy-start.1 = (f32[128,2048]{1,0:T(8,128)}, f32[128,2048]{1,0:T(8,128)S(1)}, u32[]{:S(2)}) copy-start(f32[128,2048]{1,0:T(8,128)S(1)} %get-tuple-element.15) | copy-start | bytes 3145732
  252.9 66.0 %slice-start = ((s8[5767168]{0:T(1024)(128)(4,1)}), s8[4194304]{0:T(1024)(128)(4,1)S(1)}, s32[]{:S(2)}) async-start(s8[5767168]{0:T(1024)(128)(4,1)} %bitcast.138), calls=%async_computation.7 | async-start | bytes 8388608
  254.3 64.7 %slice-start.1 = ((s8[5767168]{0:T(1024)(128)(4,1)}), s8[1572864]{0:T(1024)(128)(4,1)S(1)}, s32[]{:S(2)}) async-start(s8[5767168]{0:T(1024)(128)(4,1)} %bitcast.138), calls=%async_computation.8 | async-start | bytes 3145728
  319.0 11.0 %collective-permute-start = (bf16[64,16,2048]{2,1,0:T(8,128)(2,1)S(1)}, bf16[64,16,2048]{2,1,0:T(8,128)(2,1)S(1)}, u32[]{:S(2)}, u32[]{:S(2)}) collective-permute-start(bf16[64,16,2048]{2,1,0:T(8,128)(2,1)S(1)} %all_to_all.75), channel_id=1, source_target_pairs={{0,1},{1,0},{2,3},{3,2},{4,5},{5,4},{6,7},{7,6},{8,9},{9,8},{10,11... | collective-permute-start | bytes 12582920 | tf_op jit(solution)/shard_map/ppermute | solution.py:296
  341.4 7.5 %collective-permute-start.1 = (bf16[64,16,2048]{2,1,0:T(8,128)(2,1)S(1)}, bf16[64,16,2048]{2,1,0:T(8,128)(2,1)}, u32[]{:S(2)}, u32[]{:S(2)}) collective-permute-start(bf16[64,16,2048]{2,1,0:T(8,128)(2,1)S(1)} %convolution_convert_fusion), channel_id=1, source_target_pairs={{0,1},{1,0},{2,3},{3,2},{4,5},{5,4},{6,7},{7,6},{8,9},{9,8},{10,11... | collective-permute-start | bytes 12582920 | tf_op jit(solution)/shard_map/ppermute | solution.py:300
  354.7 8.3 %copy-start.8 = (f32[128,6]{0,1:T(8,128)S(1)}, f32[128,6]{0,1:T(8,128)}, u32[]{:S(2)}) copy-start(f32[128,6]{0,1:T(8,128)} %param.25) | copy-start | bytes 9220
  354.7 65.9 %all-to-all-start.6 = ((bf16[64,16,2048]{2,1,0:T(8,128)(2,1)}), bf16[64,16,2048]{2,1,0:T(8,128)(2,1)}, u32[]{:S(2)}, u32[]{:S(2)}) async-start(bf16[64,16,2048]{2,1,0:T(8,128)(2,1)} %add_convert_fusion), calls=%async_computation.6 | async-start | bytes 8388608 | tf_op jit(solution)/shard_map/all_to_all | solution.py:302

commit v4 on v3

--- a/solution.py
+++ b/solution.py
@@ -232,15 +232,12 @@
         ranks[None, None, :] == places[None, :, None]
     )
     picked = jnp.sum(slot_hits.astype(jnp.int32) * jnp.arange(requests, dtype=jnp.int32), axis=2)
-    filled = jnp.any(slot_hits, axis=2)
     by_dest = (offsets - my_group) % n_wide
     picked = picked[by_dest]
-    filled = filled[by_dest]
     blocks = page_pool.reshape(requests, pages_each * page_rows, kv_feat)
     outgoing = jnp.take(blocks, picked.reshape(-1), axis=0).reshape(
         n_wide, PAGE_CAP, pages_each * page_rows, kv_feat
     )
-    outgoing = jnp.where(filled[:, :, None, None], outgoing, jnp.zeros((), outgoing.dtype))
     arrived = lax.all_to_all(outgoing, "wide", split_axis=0, concat_axis=0, tiled=True)
     sources = (my_group - moves) % n_wide
     first_page = (sources * PAGE_CAP + ranks) * pages_each

time: 428 us -> 426 us (level)
    select_n x2 -> x1, other arithmetic: 4.69 us -> 0.01 us  [shards(): picked = picked[by_dest]]
    select_n x1 -> x2, other arithmetic: 0.01 us -> 4.63 us  [shards(): jnp.take(blocks, picked.reshape(-1), axis=0)]
where the time goes in v4:
time: 426 us; the launch traced here: 425 us
  waiting for transfers between devices  170 us (40%)
  blocking collectives  64.2 us (15%)
  Pallas kernels  56.1 us (13%)
  starting transfers between devices  36.7 us (9%)
  local copies, waits for them, and re-layouts  34.3 us (8%)
  matrix products  31.8 us (7%)
  other arithmetic  31.3 us (7%)
    all_to_all x1, blocking collectives, shards(): lax.all_to_all(outgoing_rows, CHIPS, split_axis=0, concat_axis=0, tiled=T...  64.2 us
    all_to_all x1, waiting for transfers between devices, shards(): lax.all_to_all(outgoing, 'wide', split_axis=0, concat_axis=0, tiled=True)  60.2 us
    all_to_all x1, waiting for transfers between devices, shards(): lax.all_to_all(summed, CHIPS, split_axis=0, concat_axis=0, tiled=True)  57.2 us
    pallas_call x1, Pallas kernels, slot_attention(): pl.pallas_call(kernel, grid_spec=grid_spec, out_shape=jax.ShapeDtypeStruc...  56.1 us
    all_to_all x1, waiting for transfers between devices, shards(): lax.all_to_all(cache_send, NARROW, split_axis=2, concat_axis=1, tiled=True)  39.5 us
    dot_general x2, matrix products, expert_apply(): both = jnp.dot(flat, expert_in[0], preferred_element_type=jnp.float32)  13.3 us
  transfers between devices with their start and end apart: 8, of which 5 were waited for; matrix products, arithmetic and copies ran while one was open for 12% of the time, Pallas kernels for 0%

profile of v4, /device:TPU:24, one launch (start us, length us, event | category | flops | bytes accessed | tf_op | source)
XLA Modules:
  0.0 425.0 jit_solution(5330227380696964252)
XLA Ops:
  2.6 4.3 %gather_fusion.3 = bf16[32,64,1024]{2,1,0:T(8,128)(2,1)} fusion(bf16[16,64,1024]{2,1,0:T(8,128)(2,1)} %bitcast.117, s32[1024]{0:T(1024)S(1)} %pad_clamp_fusion.1), kind=kCustom, calls=%fused_computation.3 | custom fusion | bytes 8388736 | tf_op jit(solution)/shard_map/jit(_take)/gather | solution.py:238
  7.0 4.6 %broadcast_select_fusion = bf16[16,2,64,1024]{3,2,1,0:T(8,128)(2,1)} fusion(bf16[16,2,64,1024]{3,2,1,0:T(8,128)(2,1)} %bitcast.115, pred[16,2]{1,0:T(8,128)(4,1)S(1)} %compare_and_fusion), kind=kLoop, calls=%fused_computation.12 | loop fusion | flops 2097152 | bytes 8388640 | tf_op jit(solution)/shard_map/jit(_take)/select_n | solution.py:238
  11.6 8.1 %all-to-all-start.2 = ((bf16[16,2,64,1024]{3,2,1,0:T(8,128)(2,1)}), bf16[16,2,64,1024]{3,2,1,0:T(8,128)(2,1)}, u32[]{:S(2)}, u32[]{:S(2)}) async-start(bf16[16,2,64,1024]{3,2,1,0:T(8,128)(2,1)} %broadcast_select_fusion), calls=%async_computation.2 | async-start | bytes 8388608 | tf_op jit(solution)/shard_map/all_to_all | solution.py:241
  21.3 60.2 %all-to-all-done.2 = bf16[16,2,64,1024]{3,2,1,0:T(8,128)(2,1)} async-done(((bf16[16,2,64,1024]{3,2,1,0:T(8,128)(2,1)}), bf16[16,2,64,1024]{3,2,1,0:T(8,128)(2,1)}, u32[]{:S(2)}, u32[]{:S(2)}) %all-to-all-start.2) | async-done | bytes 4194336 | tf_op jit(solution)/shard_map/all_to_all | solution.py:241
  81.5 4.7 %all-to-all-start = ((bf16[1,128,8,256]{1,3,0,2:T(8,128)(2,1)}), bf16[1,128,8,256]{1,3,0,2:T(8,128)(2,1)S(1)}, u32[]{:S(2)}, u32[]{:S(2)}) async-start(bf16[1,128,8,256]{1,3,0,2:T(8,128)(2,1)} %bitcast.126), calls=%async_computation | async-start | bytes 1048576 | tf_op jit(solution)/shard_map/all_to_all | solution.py:256
  93.6 4.6 %gather_fusion.5 = bf16[8,128,8,256]{3,2,1,0:T(8,128)(2,1)} fusion(bf16[128,8,4,256]{3,1,2,0:T(8,128)(2,1)} %broadcast_select_fusion.1, s32[1024]{0:T(1024)S(1)} %pad_clamp_fusion.3), kind=kCustom, calls=%fused_computation.5 | custom fusion | bytes 8388640 | tf_op jit(solution)/shard_map/jit(_take)/gather | solution.py:252
  98.2 4.6 %select_bitcast_fusion = bf16[128,8,8,256]{3,1,0,2:T(8,128)(2,1)} fusion(bf16[8,128,8,256]{3,2,1,0:T(8,128)(2,1)} %gather_fusion.5, pred[8]{0:T(512)(128)(4,1)S(1)} %compare_and_fusion.2), kind=kLoop, calls=%fused_computation.11 | loop fusion | flops 2097152 | bytes 8388616 | tf_op jit(solution)/shard_map/jit(_take)/select_n | solution.py:252
  103.6 4.8 %all-to-all-start.3 = ((bf16[128,8,8,256]{3,1,0,2:T(8,128)(2,1)}), bf16[128,8,8,256]{3,1,0,2:T(8,128)(2,1)}, u32[]{:S(2)}, u32[]{:S(2)}) async-start(bf16[128,8,8,256]{3,1,0,2:T(8,128)(2,1)} %select_bitcast_fusion), calls=%async_computation.3 | async-start | bytes 8388608 | tf_op jit(solution)/shard_map/all_to_all | solution.py:258
  116.6 39.5 %all-to-all-done.3 = bf16[128,8,8,256]{3,1,0,2:T(8,128)(2,1)} async-done(((bf16[128,8,8,256]{3,1,0,2:T(8,128)(2,1)}), bf16[128,8,8,256]{3,1,0,2:T(8,128)(2,1)}, u32[]{:S(2)}, u32[]{:S(2)}) %all-to-all-start.3) | async-done | bytes 4194336 | tf_op jit(solution)/shard_map/all_to_all | solution.py:258
  156.1 5.5 %all-to-all-start.1 = ((bf16[1,128,8,256]{3,1,0,2:T(8,128)(2,1)}), bf16[1,128,8,256]{3,1,0,2:T(8,128)(2,1)S(1)}, u32[]{:S(2)}, u32[]{:S(2)}) async-start(bf16[1,128,8,256]{3,1,0,2:T(8,128)(2,1)} %fusion.11), calls=%async_computation.1 | async-start | bytes 1048576 | tf_op jit(solution)/shard_map/all_to_all | solution.py:257
  162.3 4.4 %reduce-window.6 = s32[64,6,128]{2,0,1:T(8,128)} reduce-window(s32[64,6,128]{2,0,1:T(8,128)} %fusion.17, s32[]{:T(128)} %constant.129.clone.1), window={size=1x1x128 pad=0_0x0_0x127_0}, to_apply=%region_3.4 | reduce-window | flops 6242304 | bytes 393220 | tf_op jit(solution)/shard_map/reduce-window
  170.0 4.7 %copy.92 = bf16[128,8,8,1,256]{4,2,1,0,3:T(8,128)(2,1)} copy(bf16[128,8,8,1,256]{4,2,0,1,3:T(8,128)(2,1)} %bitcast.29) | data formatting | bytes 8388608 | tf_op jit(solution)/shard_map/all_to_all | solution.py:258
  176.6 56.1 %shard_map.136 = bf16[8,256,128]{2,1,0:T(8,128)(2,1)} custom-call(s32[168]{0:T(256)} %add.287.new_sm, s32[168]{0:T(256)} %add.291.old_sm, s32[16]{0:T(128)} %reshape.507.cnt_sm, s32[16]{0:T(128)} %bitcast.137, bf16[8,256,128]{2,1,0:T(8,128)(2,1)} %bitcast.123, s32[8,256,128]{2,1,0:T(8,128)} %broadcast_in_dim.101.segq_ref, bf16[1024,256]{1,0:T(8,128)(2,1)} %bitcast.119, ...), custom_call_target="tpu_custom_call" | custom-call | tf_op jit(solution)/shard_map/pallas_call | solution.py:183
  234.8 4.8 %all-to-all-start.4 = ((bf16[8,128,256]{1,2,0:T(8,128)(2,1)}), bf16[8,128,256]{1,2,0:T(8,128)(2,1)S(1)}, u32[]{:S(2)}, u32[]{:S(2)}) async-start(bf16[8,128,256]{1,2,0:T(8,128)(2,1)} %bitcast.127), calls=%async_computation.4 | async-start | bytes 1048576 | tf_op jit(solution)/shard_map/all_to_all | solution.py:273
  241.4 6.5 %all-to-all-done.4 = bf16[8,128,256]{1,2,0:T(8,128)(2,1)S(1)} async-done(((bf16[8,128,256]{1,2,0:T(8,128)(2,1)}), bf16[8,128,256]{1,2,0:T(8,128)(2,1)S(1)}, u32[]{:S(2)}, u32[]{:S(2)}) %all-to-all-start.4) | async-done | bytes 524320 | tf_op jit(solution)/shard_map/all_to_all | solution.py:273
  247.8 4.8 %multiply_reduce_fusion = (f32[128]{0:T(128)S(1)}, f32[128,2048]{1,0:T(8,128)S(1)}) fusion(bf16[128,2048]{0,1:T(8,128)(2,1)S(1)} %bitcast.122, bf16[2048,2048]{1,0:T(8,128)(2,1)} %param.22, bf16[128,2048]{1,0:T(8,128)(2,1)} %param.14), kind=kOutput, calls=%fused_computation.31 | convolution fusion | flops 1074790272 | bytes 10486272 | tf_op jit(solution)/shard_map/dot_general | solution.py:275
  254.0 64.2 %all_to_all.75 = bf16[64,16,2048]{2,1,0:T(8,128)(2,1)S(1)} all-to-all(bf16[64,16,2048]{2,1,0:T(8,128)(2,1)S(1)} %bitcast.116), channel_id=1, replica_groups=mesh['wide'=16,'y'=4,'core'=2] {'wide','y'}, dimensions={0} | all-to-all | bytes 8388608 | tf_op jit(solution)/shard_map/all_to_all | solution.py:291
  318.3 6.6 %fusion.2 = f32[1024,1408]{1,0:T(8,128)S(1)} fusion(bf16[1024,2048]{1,0:T(8,128)(2,1)S(1)} %bitcast.121, bf16[1,2048,1408]{2,1,0:T(8,128)(2,1)S(1)} %bitcast.139), kind=kOutput, calls=%fused_computation.9 | convolution fusion | flops 5905580032 | bytes 15728640 | tf_op jit(solution)/shard_map/dot_general | solution.py:194
  329.2 6.6 %fusion = f32[1024,1408]{1,0:T(8,128)S(1)} fusion(bf16[1024,2048]{1,0:T(8,128)(2,1)S(1)} %bitcast.140, bf16[1,2048,1408]{2,1,0:T(8,128)(2,1)S(1)} %bitcast.139), kind=kOutput, calls=%fused_computation.7 | convolution fusion | flops 5905580032 | bytes 15728640 | tf_op jit(solution)/shard_map/dot_general | solution.py:194
  341.2 6.9 %collective-permute-done.1 = bf16[64,16,2048]{2,1,0:T(8,128)(2,1)} collective-permute-done((bf16[64,16,2048]{2,1,0:T(8,128)(2,1)S(1)}, bf16[64,16,2048]{2,1,0:T(8,128)(2,1)}, u32[]{:S(2)}, u32[]{:S(2)}) %collective-permute-start.1) | collective-permute-done | bytes 4194336 | tf_op jit(solution)/shard_map/ppermute | solution.py:297
  348.1 5.9 %add_convert_fusion = bf16[64,16,2048]{2,1,0:T(8,128)(2,1)} fusion(f32[64,16,2048]{2,1,0:T(8,128)S(1)} %fusion.8, bf16[64,16,2048]{2,1,0:T(8,128)(2,1)} %collective-permute-done.1), kind=kLoop, calls=%fused_computation.6 | loop fusion | flops 6291456 | bytes 16777216 | tf_op jit(solution)/shard_map/convert_element_type | solution.py:298
  354.0 8.3 %all-to-all-start.6 = ((bf16[64,16,2048]{2,1,0:T(8,128)(2,1)}), bf16[64,16,2048]{2,1,0:T(8,128)(2,1)}, u32[]{:S(2)}, u32[]{:S(2)}) async-start(bf16[64,16,2048]{2,1,0:T(8,128)(2,1)} %add_convert_fusion), calls=%async_computation.6 | async-start | bytes 8388608 | tf_op jit(solution)/shard_map/all_to_all | solution.py:299
  362.7 57.2 %all-to-all-done.6 = bf16[64,16,2048]{2,1,0:T(8,128)(2,1)} async-done(((bf16[64,16,2048]{2,1,0:T(8,128)(2,1)}), bf16[64,16,2048]{2,1,0:T(8,128)(2,1)}, u32[]{:S(2)}, u32[]{:S(2)}) %all-to-all-start.6) | async-done | bytes 4194336 | tf_op jit(solution)/shard_map/all_to_all | solution.py:299
  419.9 5.1 %fusion.10 = bf16[128,2048]{1,0:T(8,128)(2,1)} fusion(f32[128,2048]{1,0:T(8,128)} %copy-done.1, f32[128,1024]{1,0:T(8,128)S(1)} %select_reduce_fusion, bf16[1024,2048]{1,0:T(8,128)(2,1)} %bitcast.46), kind=kOutput, calls=%fused_computation.28 | convolution fusion | flops 3221749760 | bytes 6291456 | tf_op jit(solution)/shard_map/dot_general | solution.py:303
  (102 shorter events, 41.5 us)
Async XLA Ops:
  0.0 325.8 %copy-start = (bf16[1,704,2048]{2,1,0:T(8,128)(2,1)S(1)}, bf16[1,704,2048]{2,1,0:T(8,128)(2,1)}, u32[]{:S(2)}) copy-start(bf16[1,704,2048]{2,1,0:T(8,128)(2,1)} %param.27) | copy-start | bytes 8650756
  11.6 8.1 %copy-start.10 = (s32[16]{0:T(128)S(1)}, s32[16]{0:T(128)}, u32[]{:S(2)}) copy-start(s32[16]{0:T(128)} %param.21) | copy-start | bytes 196
  11.6 8.4 %copy-start.9 = (s32[1,16,8]{1,2,0:T(8,128)S(1)}, s32[1,16,8]{1,2,0:T(8,128)}, u32[]{:S(2)}) copy-start(s32[1,16,8]{1,2,0:T(8,128)} %param.20) | copy-start | bytes 1540
  11.6 8.6 %copy-start.4 = (bf16[128,2048]{1,0:T(8,128)(2,1)S(1)}, bf16[128,2048]{1,0:T(8,128)(2,1)}, u32[]{:S(2)}) copy-start(bf16[128,2048]{1,0:T(8,128)(2,1)} %param.15) | copy-start | bytes 1572868
  11.6 69.9 %all-to-all-start.2 = ((bf16[16,2,64,1024]{3,2,1,0:T(8,128)(2,1)}), bf16[16,2,64,1024]{3,2,1,0:T(8,128)(2,1)}, u32[]{:S(2)}, u32[]{:S(2)}) async-start(bf16[16,2,64,1024]{3,2,1,0:T(8,128)(2,1)} %broadcast_select_fusion), calls=%async_computation.2 | async-start | bytes 8388608 | tf_op jit(solution)/shard_map/all_to_all | solution.py:241
  81.5 21.3 %all-to-all-start = ((bf16[1,128,8,256]{1,3,0,2:T(8,128)(2,1)}), bf16[1,128,8,256]{1,3,0,2:T(8,128)(2,1)S(1)}, u32[]{:S(2)}, u32[]{:S(2)}) async-start(bf16[1,128,8,256]{1,3,0,2:T(8,128)(2,1)} %bitcast.126), calls=%async_computation | async-start | bytes 1048576 | tf_op jit(solution)/shard_map/all_to_all | solution.py:256
  102.8 5.6 %copy-start.5 = (s32[1,1024]{1,0:T(1,128)S(1)}, s32[1,1024]{1,0:T(1,128)}, u32[]{:S(2)}) copy-start(s32[1,1024]{1,0:T(1,128)} %param.18) | copy-start | bytes 12292
  102.8 5.8 %copy-start.6 = (s32[128,6]{0,1:T(8,128)S(1)}, s32[128,6]{0,1:T(8,128)}, u32[]{:S(2)}) copy-start(s32[128,6]{0,1:T(8,128)} %param.24) | copy-start | bytes 9220
  102.8 0.8 copy-start.3
  103.6 52.5 %all-to-all-start.3 = ((bf16[128,8,8,256]{3,1,0,2:T(8,128)(2,1)}), bf16[128,8,8,256]{3,1,0,2:T(8,128)(2,1)}, u32[]{:S(2)}, u32[]{:S(2)}) async-start(bf16[128,8,8,256]{3,1,0,2:T(8,128)(2,1)} %select_bitcast_fusion), calls=%async_computation.3 | async-start | bytes 8388608 | tf_op jit(solution)/shard_map/all_to_all | solution.py:258
  156.1 18.6 %all-to-all-start.1 = ((bf16[1,128,8,256]{3,1,0,2:T(8,128)(2,1)}), bf16[1,128,8,256]{3,1,0,2:T(8,128)(2,1)S(1)}, u32[]{:S(2)}, u32[]{:S(2)}) async-start(bf16[1,128,8,256]{3,1,0,2:T(8,128)(2,1)} %fusion.11), calls=%async_computation.1 | async-start | bytes 1048576 | tf_op jit(solution)/shard_map/all_to_all | solution.py:257
  174.7 1.9 copy-start.2
  234.8 13.0 %all-to-all-start.4 = ((bf16[8,128,256]{1,2,0:T(8,128)(2,1)}), bf16[8,128,256]{1,2,0:T(8,128)(2,1)S(1)}, u32[]{:S(2)}, u32[]{:S(2)}) async-start(bf16[8,128,256]{1,2,0:T(8,128)(2,1)} %bitcast.127), calls=%async_computation.4 | async-start | bytes 1048576 | tf_op jit(solution)/shard_map/all_to_all | solution.py:273
  247.8 4.8 %copy-start.7 = (f32[2048]{0:T(1024)S(1)}, f32[2048]{0:T(1024)}, u32[]{:S(2)}) copy-start(f32[2048]{0:T(1024)} %param.23) | copy-start | bytes 24580
  252.6 65.6 %copy-start.1 = (f32[128,2048]{1,0:T(8,128)}, f32[128,2048]{1,0:T(8,128)S(1)}, u32[]{:S(2)}) copy-start(f32[128,2048]{1,0:T(8,128)S(1)} %get-tuple-element.15) | copy-start | bytes 3145732
  252.7 65.6 %slice-start = ((s8[5767168]{0:T(1024)(128)(4,1)}), s8[4194304]{0:T(1024)(128)(4,1)S(1)}, s32[]{:S(2)}) async-start(s8[5767168]{0:T(1024)(128)(4,1)} %bitcast.138), calls=%async_computation.7 | async-start | bytes 8388608
  254.0 64.2 %slice-start.1 = ((s8[5767168]{0:T(1024)(128)(4,1)}), s8[1572864]{0:T(1024)(128)(4,1)S(1)}, s32[]{:S(2)}) async-start(s8[5767168]{0:T(1024)(128)(4,1)} %bitcast.138), calls=%async_computation.8 | async-start | bytes 3145728
  318.2 11.0 %collective-permute-start = (bf16[64,16,2048]{2,1,0:T(8,128)(2,1)S(1)}, bf16[64,16,2048]{2,1,0:T(8,128)(2,1)S(1)}, u32[]{:S(2)}, u32[]{:S(2)}) collective-permute-start(bf16[64,16,2048]{2,1,0:T(8,128)(2,1)S(1)} %all_to_all.75), channel_id=1, source_target_pairs={{0,1},{1,0},{2,3},{3,2},{4,5},{5,4},{6,7},{7,6},{8,9},{9,8},{10,11... | collective-permute-start | bytes 12582920 | tf_op jit(solution)/shard_map/ppermute | solution.py:293
  340.6 7.5 %collective-permute-start.1 = (bf16[64,16,2048]{2,1,0:T(8,128)(2,1)S(1)}, bf16[64,16,2048]{2,1,0:T(8,128)(2,1)}, u32[]{:S(2)}, u32[]{:S(2)}) collective-permute-start(bf16[64,16,2048]{2,1,0:T(8,128)(2,1)S(1)} %convolution_convert_fusion), channel_id=1, source_target_pairs={{0,1},{1,0},{2,3},{3,2},{4,5},{5,4},{6,7},{7,6},{8,9},{9,8},{10,11... | collective-permute-start | bytes 12582920 | tf_op jit(solution)/shard_map/ppermute | solution.py:297
  354.0 8.3 %copy-start.8 = (f32[128,6]{0,1:T(8,128)S(1)}, f32[128,6]{0,1:T(8,128)}, u32[]{:S(2)}) copy-start(f32[128,6]{0,1:T(8,128)} %param.25) | copy-start | bytes 9220
  354.0 65.9 %all-to-all-start.6 = ((bf16[64,16,2048]{2,1,0:T(8,128)(2,1)}), bf16[64,16,2048]{2,1,0:T(8,128)(2,1)}, u32[]{:S(2)}, u32[]{:S(2)}) async-start(bf16[64,16,2048]{2,1,0:T(8,128)(2,1)} %add_convert_fusion), calls=%async_computation.6 | async-start | bytes 8388608 | tf_op jit(solution)/shard_map/all_to_all | solution.py:299

commit v5 on v4

--- a/solution.py
+++ b/solution.py
@@ -281,7 +281,11 @@
     capacity = tok_dev * TOPK * 4 // (3 * experts)
     flat_ids = expert_ids.reshape(-1)
     onehot = (flat_ids[:, None] == jnp.arange(experts, dtype=jnp.int32)[None, :]).astype(jnp.int32)
-    before = jnp.cumsum(onehot, axis=0) - onehot
+    pairs = flat_ids.shape[0]
+    earlier = (
+        lax.broadcasted_iota(jnp.int32, (pairs, pairs), 1) < lax.broadcasted_iota(jnp.int32, (pairs, pairs), 0)
+    ).astype(jnp.bfloat16)
+    before = jnp.dot(earlier, onehot.astype(jnp.bfloat16), preferred_element_type=jnp.float32).astype(jnp.int32)
     slot_place = jnp.sum(before * onehot, axis=1)
     slot_of = flat_ids * capacity + slot_place
     slot_hit = slot_of[None, :] == jnp.arange(experts * capacity, dtype=jnp.int32)[:, None]

time: 426 us -> 423 us (level)
  other arithmetic: 31.3 us -> 25.1 us
    another operation x2 -> x0, other arithmetic: 4.4 us -> none
  transfers between devices with their start and end apart: 8 -> 8, of which waited for: 5 -> 6; matrix products, arithmetic and copies ran while one was open for 12% -> 11% of each run, Pallas kernels for 0% -> 0%
where the time goes in v5:
time: 423 us; the launch traced here: 421 us
  waiting for transfers between devices  172 us (41%)
  blocking collectives  64.8 us (15%)
  Pallas kernels  56.3 us (13%)
  starting transfers between devices  37.7 us (9%)
  local copies, waits for them, and re-layouts  32.2 us (8%)
  matrix products  32.2 us (8%)
  other arithmetic  25.1 us (6%)
    all_to_all x1, blocking collectives, shards(): lax.all_to_all(outgoing_rows, CHIPS, split_axis=0, concat_axis=0, tiled=T...  64.8 us
    all_to_all x1, waiting for transfers between devices, shards(): lax.all_to_all(outgoing, 'wide', split_axis=0, concat_axis=0, tiled=True)  60.2 us
    all_to_all x1, waiting for transfers between devices, shards(): lax.all_to_all(summed, CHIPS, split_axis=0, concat_axis=0, tiled=True)  57.2 us
    pallas_call x1, Pallas kernels, slot_attention(): pl.pallas_call(kernel, grid_spec=grid_spec, out_shape=jax.ShapeDtypeStruc...  56.3 us
    all_to_all x1, waiting for transfers between devices, shards(): lax.all_to_all(cache_send, NARROW, split_axis=2, concat_axis=1, tiled=True)  40.6 us
    dot_general x2, matrix products, expert_apply(): both = jnp.dot(flat, expert_in[0], preferred_element_type=jnp.float32)  13.3 us
  transfers between devices with their start and end apart: 8, of which 6 were waited for; matrix products, arithmetic and copies ran while one was open for 11% of the time, Pallas kernels for 0%

profile of v5, /device:TPU:24, one launch (start us, length us, event | category | flops | bytes accessed | tf_op | source)
XLA Modules:
  0.0 421.1 jit_solution(6013655048607718658)
XLA Ops:
  2.6 4.4 %gather_fusion.3 = bf16[32,64,1024]{2,1,0:T(8,128)(2,1)} fusion(bf16[16,64,1024]{2,1,0:T(8,128)(2,1)} %bitcast.97, s32[1024]{0:T(1024)S(1)} %pad_clamp_fusion.1), kind=kCustom, calls=%fused_computation.3 | custom fusion | bytes 8388736 | tf_op jit(solution)/shard_map/jit(_take)/gather | solution.py:238
  7.0 4.6 %broadcast_select_fusion = bf16[16,2,64,1024]{3,2,1,0:T(8,128)(2,1)} fusion(bf16[16,2,64,1024]{3,2,1,0:T(8,128)(2,1)} %bitcast.95, pred[16,2]{1,0:T(8,128)(4,1)S(1)} %compare_and_fusion), kind=kLoop, calls=%fused_computation.12 | loop fusion | flops 2097152 | bytes 8388640 | tf_op jit(solution)/shard_map/jit(_take)/select_n | solution.py:238
  11.6 8.1 %all-to-all-start.2 = ((bf16[16,2,64,1024]{3,2,1,0:T(8,128)(2,1)}), bf16[16,2,64,1024]{3,2,1,0:T(8,128)(2,1)}, u32[]{:S(2)}, u32[]{:S(2)}) async-start(bf16[16,2,64,1024]{3,2,1,0:T(8,128)(2,1)} %broadcast_select_fusion), calls=%async_computation.2 | async-start | bytes 8388608 | tf_op jit(solution)/shard_map/all_to_all | solution.py:241
  21.3 60.2 %all-to-all-done.2 = bf16[16,2,64,1024]{3,2,1,0:T(8,128)(2,1)} async-done(((bf16[16,2,64,1024]{3,2,1,0:T(8,128)(2,1)}), bf16[16,2,64,1024]{3,2,1,0:T(8,128)(2,1)}, u32[]{:S(2)}, u32[]{:S(2)}) %all-to-all-start.2) | async-done | bytes 4194336 | tf_op jit(solution)/shard_map/all_to_all | solution.py:241
  81.5 4.7 %all-to-all-start = ((bf16[1,128,8,256]{1,3,0,2:T(8,128)(2,1)}), bf16[1,128,8,256]{1,3,0,2:T(8,128)(2,1)S(1)}, u32[]{:S(2)}, u32[]{:S(2)}) async-start(bf16[1,128,8,256]{1,3,0,2:T(8,128)(2,1)} %bitcast.106), calls=%async_computation | async-start | bytes 1048576 | tf_op jit(solution)/shard_map/all_to_all | solution.py:256
  86.2 4.2 gather_fusion.4
  93.6 4.6 %gather_fusion.5 = bf16[8,128,8,256]{3,2,1,0:T(8,128)(2,1)} fusion(bf16[128,8,4,256]{3,1,2,0:T(8,128)(2,1)} %broadcast_select_fusion.1, s32[1024]{0:T(1024)S(1)} %pad_clamp_fusion.3), kind=kCustom, calls=%fused_computation.5 | custom fusion | bytes 8388640 | tf_op jit(solution)/shard_map/jit(_take)/gather | solution.py:252
  98.2 4.6 %select_bitcast_fusion = bf16[128,8,8,256]{3,1,0,2:T(8,128)(2,1)} fusion(bf16[8,128,8,256]{3,2,1,0:T(8,128)(2,1)} %gather_fusion.5, pred[8]{0:T(512)(128)(4,1)S(1)} %compare_and_fusion.2), kind=kLoop, calls=%fused_computation.11 | loop fusion | flops 2097152 | bytes 8388616 | tf_op jit(solution)/shard_map/jit(_take)/select_n | solution.py:252
  102.8 4.9 %all-to-all-start.3 = ((bf16[128,8,8,256]{3,1,0,2:T(8,128)(2,1)}), bf16[128,8,8,256]{3,1,0,2:T(8,128)(2,1)}, u32[]{:S(2)}, u32[]{:S(2)}) async-start(bf16[128,8,8,256]{3,1,0,2:T(8,128)(2,1)} %select_bitcast_fusion), calls=%async_computation.3 | async-start | bytes 8388608 | tf_op jit(solution)/shard_map/all_to_all | solution.py:258
  114.8 40.6 %all-to-all-done.3 = bf16[128,8,8,256]{3,1,0,2:T(8,128)(2,1)} async-done(((bf16[128,8,8,256]{3,1,0,2:T(8,128)(2,1)}), bf16[128,8,8,256]{3,1,0,2:T(8,128)(2,1)}, u32[]{:S(2)}, u32[]{:S(2)}) %all-to-all-start.3) | async-done | bytes 4194336 | tf_op jit(solution)/shard_map/all_to_all | solution.py:258
  155.4 5.5 %all-to-all-start.1 = ((bf16[1,128,8,256]{3,1,0,2:T(8,128)(2,1)}), bf16[1,128,8,256]{3,1,0,2:T(8,128)(2,1)S(1)}, u32[]{:S(2)}, u32[]{:S(2)}) async-start(bf16[1,128,8,256]{3,1,0,2:T(8,128)(2,1)} %fusion.15), calls=%async_computation.1 | async-start | bytes 1048576 | tf_op jit(solution)/shard_map/all_to_all | solution.py:257
  164.0 4.7 %copy.84 = bf16[128,8,8,1,256]{4,2,1,0,3:T(8,128)(2,1)} copy(bf16[128,8,8,1,256]{4,2,0,1,3:T(8,128)(2,1)} %bitcast.29) | data formatting | bytes 8388608 | tf_op jit(solution)/shard_map/all_to_all | solution.py:258
  171.1 56.3 %shard_map.136 = bf16[8,256,128]{2,1,0:T(8,128)(2,1)} custom-call(s32[168]{0:T(256)} %add.287.new_sm, s32[168]{0:T(256)} %add.291.old_sm, s32[16]{0:T(128)} %reshape.491.cnt_sm, s32[16]{0:T(128)} %bitcast.116, bf16[8,256,128]{2,1,0:T(8,128)(2,1)} %bitcast.103, s32[8,256,128]{2,1,0:T(8,128)} %broadcast_in_dim.101.segq_ref, bf16[1024,256]{1,0:T(8,128)(2,1)} %bitcast.99, ...), custom_call_target="tpu_custom_call" | custom-call | tf_op jit(solution)/shard_map/pallas_call | solution.py:183
  229.5 5.5 %all-to-all-start.4 = ((bf16[8,128,256]{1,2,0:T(8,128)(2,1)}), bf16[8,128,256]{1,2,0:T(8,128)(2,1)S(1)}, u32[]{:S(2)}, u32[]{:S(2)}) async-start(bf16[8,128,256]{1,2,0:T(8,128)(2,1)} %bitcast.107), calls=%async_computation.4 | async-start | bytes 1048576 | tf_op jit(solution)/shard_map/all_to_all | solution.py:273
  236.1 7.1 %all-to-all-done.4 = bf16[8,128,256]{1,2,0:T(8,128)(2,1)S(1)} async-done(((bf16[8,128,256]{1,2,0:T(8,128)(2,1)}), bf16[8,128,256]{1,2,0:T(8,128)(2,1)S(1)}, u32[]{:S(2)}, u32[]{:S(2)}) %all-to-all-start.4) | async-done | bytes 524320 | tf_op jit(solution)/shard_map/all_to_all | solution.py:273
  243.2 4.8 %multiply_reduce_fusion = (f32[128]{0:T(128)S(1)}, f32[128,2048]{1,0:T(8,128)S(1)}) fusion(bf16[128,2048]{0,1:T(8,128)(2,1)S(1)} %bitcast.102, bf16[2048,2048]{1,0:T(8,128)(2,1)} %param.22, bf16[128,2048]{1,0:T(8,128)(2,1)} %param.14), kind=kOutput, calls=%fused_computation.36 | convolution fusion | flops 1074790272 | bytes 10486272 | tf_op jit(solution)/shard_map/dot_general | solution.py:275
  249.4 64.8 %all_to_all.75 = bf16[64,16,2048]{2,1,0:T(8,128)(2,1)S(1)} all-to-all(bf16[64,16,2048]{2,1,0:T(8,128)(2,1)S(1)} %bitcast.96), channel_id=1, replica_groups=mesh['wide'=16,'y'=4,'core'=2] {'wide','y'}, dimensions={0} | all-to-all | bytes 8388608 | tf_op jit(solution)/shard_map/all_to_all | solution.py:295
  314.3 6.6 %fusion.2 = f32[1024,1408]{1,0:T(8,128)S(1)} fusion(bf16[1024,2048]{1,0:T(8,128)(2,1)S(1)} %bitcast.101, bf16[1,2048,1408]{2,1,0:T(8,128)(2,1)S(1)} %bitcast.118), kind=kOutput, calls=%fused_computation.9 | convolution fusion | flops 5905580032 | bytes 15728640 | tf_op jit(solution)/shard_map/dot_general | solution.py:194
  325.3 6.6 %fusion = f32[1024,1408]{1,0:T(8,128)S(1)} fusion(bf16[1024,2048]{1,0:T(8,128)(2,1)S(1)} %bitcast.119, bf16[1,2048,1408]{2,1,0:T(8,128)(2,1)S(1)} %bitcast.118), kind=kOutput, calls=%fused_computation.7 | convolution fusion | flops 5905580032 | bytes 15728640 | tf_op jit(solution)/shard_map/dot_general | solution.py:194
  337.2 6.9 %collective-permute-done.1 = bf16[64,16,2048]{2,1,0:T(8,128)(2,1)} collective-permute-done((bf16[64,16,2048]{2,1,0:T(8,128)(2,1)S(1)}, bf16[64,16,2048]{2,1,0:T(8,128)(2,1)}, u32[]{:S(2)}, u32[]{:S(2)}) %collective-permute-start.1) | collective-permute-done | bytes 4194336 | tf_op jit(solution)/shard_map/ppermute | solution.py:301
  344.1 5.8 %add_convert_fusion = bf16[64,16,2048]{2,1,0:T(8,128)(2,1)} fusion(f32[64,16,2048]{2,1,0:T(8,128)S(1)} %fusion.8, bf16[64,16,2048]{2,1,0:T(8,128)(2,1)} %collective-permute-done.1), kind=kLoop, calls=%fused_computation.6 | loop fusion | flops 6291456 | bytes 16777216 | tf_op jit(solution)/shard_map/convert_element_type | solution.py:302
  350.0 8.4 %all-to-all-start.6 = ((bf16[64,16,2048]{2,1,0:T(8,128)(2,1)}), bf16[64,16,2048]{2,1,0:T(8,128)(2,1)}, u32[]{:S(2)}, u32[]{:S(2)}) async-start(bf16[64,16,2048]{2,1,0:T(8,128)(2,1)} %add_convert_fusion), calls=%async_computation.6 | async-start | bytes 8388608 | tf_op jit(solution)/shard_map/all_to_all | solution.py:303
  358.8 57.2 %all-to-all-done.6 = bf16[64,16,2048]{2,1,0:T(8,128)(2,1)} async-done(((bf16[64,16,2048]{2,1,0:T(8,128)(2,1)}), bf16[64,16,2048]{2,1,0:T(8,128)(2,1)}, u32[]{:S(2)}, u32[]{:S(2)}) %all-to-all-start.6) | async-done | bytes 4194336 | tf_op jit(solution)/shard_map/all_to_all | solution.py:303
  416.0 5.1 %fusion.10 = bf16[128,2048]{1,0:T(8,128)(2,1)} fusion(f32[128,2048]{1,0:T(8,128)} %copy-done.1, f32[128,1024]{1,0:T(8,128)S(1)} %select_reduce_fusion, bf16[1024,2048]{1,0:T(8,128)(2,1)} %bitcast.45), kind=kOutput, calls=%fused_computation.28 | convolution fusion | flops 3221749760 | bytes 6291456 | tf_op jit(solution)/shard_map/dot_general | solution.py:307
  (97 shorter events, 34.3 us)
Async XLA Ops:
  0.0 321.8 %copy-start = (bf16[1,704,2048]{2,1,0:T(8,128)(2,1)S(1)}, bf16[1,704,2048]{2,1,0:T(8,128)(2,1)}, u32[]{:S(2)}) copy-start(bf16[1,704,2048]{2,1,0:T(8,128)(2,1)} %param.27) | copy-start | bytes 8650756
  11.6 8.1 %copy-start.10 = (s32[16]{0:T(128)S(1)}, s32[16]{0:T(128)}, u32[]{:S(2)}) copy-start(s32[16]{0:T(128)} %param.21) | copy-start | bytes 196
  11.6 8.4 %copy-start.9 = (s32[1,16,8]{1,2,0:T(8,128)S(1)}, s32[1,16,8]{1,2,0:T(8,128)}, u32[]{:S(2)}) copy-start(s32[1,16,8]{1,2,0:T(8,128)} %param.20) | copy-start | bytes 1540
  11.6 8.6 %copy-start.4 = (bf16[128,2048]{1,0:T(8,128)(2,1)S(1)}, bf16[128,2048]{1,0:T(8,128)(2,1)}, u32[]{:S(2)}) copy-start(bf16[128,2048]{1,0:T(8,128)(2,1)} %param.15) | copy-start | bytes 1572868
  11.6 69.9 %all-to-all-start.2 = ((bf16[16,2,64,1024]{3,2,1,0:T(8,128)(2,1)}), bf16[16,2,64,1024]{3,2,1,0:T(8,128)(2,1)}, u32[]{:S(2)}, u32[]{:S(2)}) async-start(bf16[16,2,64,1024]{3,2,1,0:T(8,128)(2,1)} %broadcast_select_fusion), calls=%async_computation.2 | async-start | bytes 8388608 | tf_op jit(solution)/shard_map/all_to_all | solution.py:241
  81.5 21.3 %all-to-all-start = ((bf16[1,128,8,256]{1,3,0,2:T(8,128)(2,1)}), bf16[1,128,8,256]{1,3,0,2:T(8,128)(2,1)S(1)}, u32[]{:S(2)}, u32[]{:S(2)}) async-start(bf16[1,128,8,256]{1,3,0,2:T(8,128)(2,1)} %bitcast.106), calls=%async_computation | async-start | bytes 1048576 | tf_op jit(solution)/shard_map/all_to_all | solution.py:256
  102.8 5.0 %copy-start.5 = (s32[1,1024]{1,0:T(1,128)S(1)}, s32[1,1024]{1,0:T(1,128)}, u32[]{:S(2)}) copy-start(s32[1,1024]{1,0:T(1,128)} %param.18) | copy-start | bytes 12292
  102.8 4.9 %copy-start.3 = (bf16[1,128,8,256]{1,3,0,2:T(8,128)(2,1)}, bf16[1,128,8,256]{1,3,0,2:T(8,128)(2,1)S(1)}, u32[]{:S(2)}) copy-start(bf16[1,128,8,256]{1,3,0,2:T(8,128)(2,1)S(1)} %all-to-all-done) | copy-start | bytes 1572868
  102.8 52.6 %all-to-all-start.3 = ((bf16[128,8,8,256]{3,1,0,2:T(8,128)(2,1)}), bf16[128,8,8,256]{3,1,0,2:T(8,128)(2,1)}, u32[]{:S(2)}, u32[]{:S(2)}) async-start(bf16[128,8,8,256]{3,1,0,2:T(8,128)(2,1)} %select_bitcast_fusion), calls=%async_computation.3 | async-start | bytes 8388608 | tf_op jit(solution)/shard_map/all_to_all | solution.py:258
  107.8 53.9 %copy-start.6 = (s32[128,6]{0,1:T(8,128)S(1)}, s32[128,6]{0,1:T(8,128)}, u32[]{:S(2)}) copy-start(s32[128,6]{0,1:T(8,128)} %param.24) | copy-start | bytes 9220
  155.4 13.7 %all-to-all-start.1 = ((bf16[1,128,8,256]{3,1,0,2:T(8,128)(2,1)}), bf16[1,128,8,256]{3,1,0,2:T(8,128)(2,1)S(1)}, u32[]{:S(2)}, u32[]{:S(2)}) async-start(bf16[1,128,8,256]{3,1,0,2:T(8,128)(2,1)} %fusion.15), calls=%async_computation.1 | async-start | bytes 1048576 | tf_op jit(solution)/shard_map/all_to_all | solution.py:257
  169.2 1.9 copy-start.2
  229.5 13.7 %all-to-all-start.4 = ((bf16[8,128,256]{1,2,0:T(8,128)(2,1)}), bf16[8,128,256]{1,2,0:T(8,128)(2,1)S(1)}, u32[]{:S(2)}, u32[]{:S(2)}) async-start(bf16[8,128,256]{1,2,0:T(8,128)(2,1)} %bitcast.107), calls=%async_computation.4 | async-start | bytes 1048576 | tf_op jit(solution)/shard_map/all_to_all | solution.py:273
  243.2 4.8 %copy-start.7 = (f32[2048]{0:T(1024)S(1)}, f32[2048]{0:T(1024)}, u32[]{:S(2)}) copy-start(f32[2048]{0:T(1024)} %param.23) | copy-start | bytes 24580
  248.0 66.2 %copy-start.1 = (f32[128,2048]{1,0:T(8,128)}, f32[128,2048]{1,0:T(8,128)S(1)}, u32[]{:S(2)}) copy-start(f32[128,2048]{1,0:T(8,128)S(1)} %get-tuple-element.15) | copy-start | bytes 3145732
  248.1 66.2 %slice-start = ((s8[5767168]{0:T(1024)(128)(4,1)}), s8[4194304]{0:T(1024)(128)(4,1)S(1)}, s32[]{:S(2)}) async-start(s8[5767168]{0:T(1024)(128)(4,1)} %bitcast.117), calls=%async_computation.7 | async-start | bytes 8388608
  249.4 64.9 %slice-start.1 = ((s8[5767168]{0:T(1024)(128)(4,1)}), s8[1572864]{0:T(1024)(128)(4,1)S(1)}, s32[]{:S(2)}) async-start(s8[5767168]{0:T(1024)(128)(4,1)} %bitcast.117), calls=%async_computation.8 | async-start | bytes 3145728
  314.3 11.0 %collective-permute-start = (bf16[64,16,2048]{2,1,0:T(8,128)(2,1)S(1)}, bf16[64,16,2048]{2,1,0:T(8,128)(2,1)S(1)}, u32[]{:S(2)}, u32[]{:S(2)}) collective-permute-start(bf16[64,16,2048]{2,1,0:T(8,128)(2,1)S(1)} %all_to_all.75), channel_id=1, source_target_pairs={{0,1},{1,0},{2,3},{3,2},{4,5},{5,4},{6,7},{7,6},{8,9},{9,8},{10,11... | collective-permute-start | bytes 12582920 | tf_op jit(solution)/shard_map/ppermute | solution.py:297
  336.7 7.5 %collective-permute-start.1 = (bf16[64,16,2048]{2,1,0:T(8,128)(2,1)S(1)}, bf16[64,16,2048]{2,1,0:T(8,128)(2,1)}, u32[]{:S(2)}, u32[]{:S(2)}) collective-permute-start(bf16[64,16,2048]{2,1,0:T(8,128)(2,1)S(1)} %convolution_convert_fusion), channel_id=1, source_target_pairs={{0,1},{1,0},{2,3},{3,2},{4,5},{5,4},{6,7},{7,6},{8,9},{9,8},{10,11... | collective-permute-start | bytes 12582920 | tf_op jit(solution)/shard_map/ppermute | solution.py:301
  350.0 8.4 %copy-start.8 = (f32[128,6]{0,1:T(8,128)S(1)}, f32[128,6]{0,1:T(8,128)}, u32[]{:S(2)}) copy-start(f32[128,6]{0,1:T(8,128)} %param.25) | copy-start | bytes 9220
  350.0 66.0 %all-to-all-start.6 = ((bf16[64,16,2048]{2,1,0:T(8,128)(2,1)}), bf16[64,16,2048]{2,1,0:T(8,128)(2,1)}, u32[]{:S(2)}, u32[]{:S(2)}) async-start(bf16[64,16,2048]{2,1,0:T(8,128)(2,1)} %add_convert_fusion), calls=%async_computation.6 | async-start | bytes 8388608 | tf_op jit(solution)/shard_map/all_to_all | solution.py:303
